TPU v7x, 256 devices: a whole 4x4x8 slice. The times are simulated.
256 devices in a mesh: section: 8 (over z), joint: 32 (over y, x, core).
Axes of the slice: x: 4, y: 4, z: 8, core: 2. Of those that a mesh axis runs over, the one named last changes fastest.
Arguments:
- encoder_rows: bfloat16 [32, 1024, 1536], P('joint', 'section'), may hold values from -6 to 6
- up_weight: bfloat16 [1536, 3072], P(None, 'section'), may hold values from -0.15625 to 0.15625
- down_weight: bfloat16 [3072, 1536], P('section'), may hold values from -0.109375 to 0.109375
- encoder_proj: bfloat16 [1536, 640], replicated, may hold values from -0.15625 to 0.15625
- embedding: bfloat16 [4096, 640], P('joint'), may hold values from -6 to 6
- conv_taps: float32 [2, 640], replicated, may hold values from -3 to 3
- decoder_proj: bfloat16 [640, 640], replicated, may hold values from -0.25 to 0.25
- output_proj: bfloat16 [640, 4096], replicated, may hold values from -0.5 to 0.5
- output_bias: float32 [4096], replicated, may hold values from -6 to 6
- frame_lengths: int32 [32], replicated, may hold values from 1 to 1024, 20480 in all
- label_lengths: int32 [32], replicated, may hold values from 1 to 3, 48 in all
- label_ids: int32 [32, 3], replicated, may hold values from 1 to 4095
- owner_index: int32 [32], replicated, may hold values from 0 to 31, each once
Outputs:
- enc_grad: bfloat16 [32, 1024, 1536], P('joint', 'section')
- up_grad: float32 [1536, 3072], P('joint', 'section')
- down_grad: float32 [3072, 1536], P('section', 'joint')
- pred_grad: float32 [32, 4, 640], P('joint', None, 'section')
Inputs may be any that keep to these rules, and one draw needn't show every extreme that they name: `owner_index`: every joint owner receives exactly one utterance. `frame_lengths`: the longest utterance uses all 1024 frames. `label_lengths`: the longest label sequence has 3 labels. `label_ids`: never the blank token 0.
All inputs are finite; a program needn't handle non-finite values.
Results may differ from a plain program's by a relative error of at most 0.013.
Values may be sent and summed in bfloat16 or wider, within the bound.
No kernel may reach another device: no remote copies, remote signals or barrier semaphores. Data moves between devices by JAX's collectives and lax.ppermute only.
A program may use at most 128 MiB of HBM per device.

v0:
```python
import jax
import jax.numpy as jnp
from jax import lax
from jax.sharding import PartitionSpec as P

NEG_BIG = -1000000000.0


def partner_2(block, axis, bit):
    count = lax.axis_size(axis)
    route = []
    for low in range(count):
        high = low | 1 << bit
        if high != low and high < count:
            route += [(low, high), (high, low)]
    return lax.ppermute(block, axis, route)


def from_behind(value, axis, steps):
    count = lax.axis_size(axis)
    initial, last = (max(0, -steps), min(count, count - steps))
    return lax.ppermute(value, axis, [(source, source + steps) for source in range(initial, last)])


def layer_norm(values):
    average = jnp.mean(values, axis=-1, keepdims=True)
    centered = values - average
    variance = jnp.mean(centered * centered, axis=-1, keepdims=True)
    inv_scale = lax.rsqrt(variance + 1e-05)
    return (centered * inv_scale, inv_scale)


def lower_paths(label_row):
    partial_sums = jnp.concatenate([jnp.zeros((1,), jnp.float32), jnp.cumsum(label_row)])
    places = partial_sums.shape[0]
    row_ids = lax.broadcasted_iota(jnp.int32, (places, places), 0)
    col_ids = lax.broadcasted_iota(jnp.int32, (places, places), 1)
    return jnp.where(col_ids <= row_ids, partial_sums[:, None] - partial_sums[None, :], NEG_BIG)


def advance(vector, blank_row, label_row, active):
    moved = blank_row + jax.nn.logsumexp(lower_paths(label_row) + vector[None, :], axis=1)
    return jnp.where(active, moved, vector)


def run_block(vector, blank_score, label_score, active):

    def run_one_frame(carried, inputs):
        blank_row, label_row, live_flag = inputs
        return (advance(carried, blank_row, label_row, live_flag), None)

    return lax.scan(run_one_frame, vector, (blank_score, label_score, active))[0]


def block_matrix(blank_score, label_score, active):
    places = blank_score.shape[1]
    row_ids = lax.broadcasted_iota(jnp.int32, (places, places), 0)
    col_ids = lax.broadcasted_iota(jnp.int32, (places, places), 1)
    identity_map = jnp.where(row_ids == col_ids, 0.0, NEG_BIG)

    def block_one_frame(carried, inputs):
        blank_row, label_row, live_flag = inputs
        moved = blank_row[:, None] + jax.nn.logsumexp(
            lower_paths(label_row)[:, :, None] + carried[None, :, :], axis=1
        )
        return (jnp.where(live_flag, moved, carried), None)

    return lax.scan(block_one_frame, identity_map, (blank_score, label_score, active))[0]


def log_apply(transfer, vector):
    return jax.nn.logsumexp(transfer + vector[None, :], axis=1)


def log_apply_back(transfer, vector):
    return jax.nn.logsumexp(transfer + vector[:, None], axis=0)


def joint_forward(frame_part, pred_here, label_row_ids, output_proj, output_bias):
    joined = jnp.tanh(frame_part.astype(jnp.float32)[:, None, :] + pred_here[None, :, :]).astype(
        jnp.bfloat16
    )
    frames_here, places, joint_width = joined.shape
    logits = (
        jnp.dot(
            joined.reshape(frames_here * places, joint_width),
            output_proj,
            preferred_element_type=jnp.float32,
        )
        + output_bias
    )
    logits = logits.reshape(frames_here, places, -1)
    exponent = jnp.exp(logits)
    denominator = jnp.sum(exponent, axis=-1, keepdims=True)
    log_total = jnp.log(denominator)[:, :, 0]
    blank_score = logits[:, :, 0] - log_total
    index_grid = jnp.broadcast_to(label_row_ids[None, :, None], (frames_here, places - 1, 1))
    picked = jnp.take_along_axis(logits[:, :-1, :], index_grid, axis=2)[:, :, 0]
    label_score = picked - log_total[:, :-1]
    posterior = exponent / denominator
    return (joined, posterior, blank_score, label_score)


def joint_backward(blank_grad, label_grad, label_row_ids, joined, posterior, output_proj):
    frames_here, places, vocab_size = posterior.shape
    label_full = jnp.pad(label_grad, ((0, 0), (0, 1)))
    weight_sum = blank_grad + label_full
    token_full = jnp.concatenate([label_row_ids, jnp.full((1,), -1, jnp.int32)])
    vocab_iota = lax.broadcasted_iota(jnp.int32, (1, 1, vocab_size), 2)
    blank_term = jnp.where(vocab_iota == 0, blank_grad[:, :, None], 0.0)
    label_term = jnp.where(vocab_iota == token_full[None, :, None], label_full[:, :, None], 0.0)
    logit_grad = -posterior * weight_sum[:, :, None] + blank_term + label_term
    logit_grad = logit_grad.astype(jnp.bfloat16).reshape(frames_here * places, vocab_size)
    joined_grad = lax.dot_general(
        logit_grad, output_proj, (((1,), (1,)), ((), ())), preferred_element_type=jnp.float32
    )
    joined_vals = joined.astype(jnp.float32).reshape(frames_here * places, -1)
    inner_grad = (joined_grad * (1.0 - joined_vals * joined_vals)).reshape(frames_here, places, -1)
    frame_part_grad = jnp.sum(inner_grad, axis=1).astype(jnp.bfloat16)
    pred_part_grad = jnp.sum(inner_grad, axis=0)
    return (frame_part_grad, pred_part_grad)


def network_sections(count):
    sections = []
    block_size = 2
    while block_size <= count:
        stride = block_size // 2
        while stride >= 1:
            sections.append((block_size, stride))
            stride = stride // 2
        block_size = block_size * 2
    return sections


def sort_section(keys, block_size, stride, device_id):
    count = keys.shape[0]
    position = jnp.arange(count, dtype=jnp.int32)
    partner = position ^ stride
    partner_keys = keys[partner]
    rising = position & block_size == 0
    lower_side = position < partner
    keep_small = lower_side == rising
    new_keys = jnp.where(
        keep_small, jnp.minimum(keys, partner_keys), jnp.maximum(keys, partner_keys)
    )
    takes = new_keys[device_id] != keys[device_id]
    return (new_keys, takes)


def route_owner(payload, keys, device_id, count):
    for block_size, stride in network_sections(count):
        keys, takes = sort_section(keys, block_size, stride, device_id)
        other = partner_2(payload, "joint", stride.bit_length() - 1)
        payload = jnp.where(takes, other, payload)
    return payload


def route_holder(payload, keys, device_id, count):
    for block_size, stride in network_sections(count):
        keys, takes = sort_section(keys, block_size, stride, device_id)
        other = partner_2(payload, "joint", stride.bit_length() - 1)
        payload = jnp.where(takes, other, payload)
    return payload


def on_device(
    encoder_rows,
    up_weight,
    down_weight,
    encoder_proj,
    embedding,
    conv_taps,
    decoder_proj,
    output_proj,
    output_bias,
    frame_lengths,
    label_lengths,
    label_ids,
    owner_index,
):
    section_count = lax.axis_size("section")
    joint_count = lax.axis_size("joint")
    section_id = lax.axis_index("section")
    joint_id = lax.axis_index("joint")
    block_len = encoder_rows.shape[1]
    utterances = label_ids.shape[0]
    places = label_ids.shape[1] + 1
    own_rows = encoder_rows[0].astype(jnp.float32)
    normed_in = layer_norm(own_rows)[0].astype(jnp.bfloat16)
    gathered = lax.all_gather(normed_in, "section", axis=0, tiled=True)
    pre_hidden = jnp.dot(gathered, up_weight, preferred_element_type=jnp.float32)
    hidden = jax.nn.silu(pre_hidden).astype(jnp.bfloat16)
    encoded = own_rows + lax.psum_scatter(
        0.5 * jnp.dot(hidden, down_weight, preferred_element_type=jnp.float32),
        "section",
        scatter_dimension=0,
        tiled=True,
    )
    unit_rows, inv_scale = layer_norm(encoded)
    frame_part = jnp.dot(
        unit_rows.astype(jnp.bfloat16), encoder_proj, preferred_element_type=jnp.float32
    ).astype(jnp.bfloat16)
    order_iota = jnp.arange(utterances, dtype=jnp.int32)
    inverse = jnp.zeros((utterances,), jnp.int32).at[owner_index].set(order_iota)
    own_utterance = inverse[joint_id]
    owner_frames = route_owner(frame_part, owner_index, joint_id, joint_count)
    context = jnp.concatenate([jnp.zeros((utterances, 1), jnp.int32), label_ids], axis=1)
    vocab_rows = embedding.shape[0]
    vocab_ids = joint_id * vocab_rows + jnp.arange(vocab_rows, dtype=jnp.int32)

    def label_term(start_row, row_count):
        number = row_count // places
        wanted = context[inverse].reshape(number * places)
        selector = (wanted[:, None] == vocab_ids[None, :]).astype(jnp.bfloat16)
        return jnp.dot(selector, embedding, preferred_element_type=jnp.float32)

    looked = lax.psum_scatter(
        label_term(jnp.int32(0), places * lax.axis_size("joint")).astype(jnp.bfloat16),
        "joint",
        scatter_dimension=0,
        tiled=True,
    ).astype(jnp.float32)
    previous = jnp.concatenate([looked[:1], looked[:-1]], axis=0)
    pred_act = jnp.maximum(conv_taps[0] * previous + conv_taps[1] * looked, 0.0).astype(
        jnp.bfloat16
    )
    pred_rows = jnp.dot(pred_act, decoder_proj, preferred_element_type=jnp.float32)
    label_here = label_ids[own_utterance]
    frames_used = frame_lengths[own_utterance]
    labels_used = label_lengths[own_utterance]
    joined, posterior, blank_score, label_score = joint_forward(
        owner_frames, pred_rows, label_here, output_proj, output_bias
    )
    frame_ids = section_id * block_len + jnp.arange(block_len, dtype=jnp.int32)
    active = frame_ids < frames_used
    transfer = block_matrix(blank_score, label_score, active)
    place_iota = jnp.arange(places, dtype=jnp.int32)
    start_vec = jnp.where(place_iota == 0, 0.0, NEG_BIG)
    finish_vec = jnp.where(place_iota == labels_used, 0.0, NEG_BIG)

    def forward_turn(turn_index, carried):
        passed = from_behind(log_apply(transfer, carried), "section", 1)
        return jnp.where(section_id == 0, start_vec, passed)

    incoming = lax.fori_loop(0, section_count - 1, forward_turn, start_vec)

    def backward_turn(turn_index, carried):
        passed = from_behind(log_apply_back(transfer, carried), "section", -1)
        return jnp.where(section_id == section_count - 1, finish_vec, passed)

    leaving = lax.fori_loop(0, section_count - 1, backward_turn, finish_vec)

    def block_out(blank_in, label_in):
        return run_block(incoming, blank_in, label_in, active)

    end_alpha, pullback = jax.vjp(block_out, blank_score, label_score)
    logprob = jax.nn.logsumexp(end_alpha + leaving)
    blank_grad, label_grad = pullback(-jnp.exp(end_alpha + leaving - logprob))
    frame_part_grad, pred_part = joint_backward(
        blank_grad, label_grad, label_here, joined, posterior, output_proj
    )
    part_grad = route_holder(frame_part_grad, inverse, joint_id, joint_count)
    unit_grad = lax.dot_general(
        part_grad, encoder_proj, (((1,), (1,)), ((), ())), preferred_element_type=jnp.float32
    )
    first_mean = jnp.mean(unit_grad, axis=-1, keepdims=True)
    second_mean = jnp.mean(unit_grad * unit_rows, axis=-1, keepdims=True)
    row_grad = (inv_scale * (unit_grad - first_mean - unit_rows * second_mean)).astype(jnp.bfloat16)
    grad_all = lax.all_gather(row_grad, "section", axis=0, tiled=True)
    hidden_grad = 0.5 * lax.dot_general(
        grad_all, down_weight, (((1,), (1,)), ((), ())), preferred_element_type=jnp.float32
    )
    gate_sigmoid = jax.nn.sigmoid(pre_hidden)
    pre_grad = (hidden_grad * gate_sigmoid * (1.0 + pre_hidden * (1.0 - gate_sigmoid))).astype(
        jnp.bfloat16
    )
    up_part = lax.dot_general(
        gathered, pre_grad, (((0,), (0,)), ((), ())), preferred_element_type=jnp.float32
    )
    down_part = 0.5 * lax.dot_general(
        hidden, grad_all, (((0,), (0,)), ((), ())), preferred_element_type=jnp.float32
    )
    up_sum, down_sum = (
        lax.psum_scatter(
            up_part.astype(jnp.bfloat16), "joint", scatter_dimension=0, tiled=True
        ).astype(jnp.float32),
        lax.psum_scatter(
            down_part.astype(jnp.bfloat16), "joint", scatter_dimension=1, tiled=True
        ).astype(jnp.float32),
    )
    pred_sum = lax.psum_scatter(pred_part[None], "section", scatter_dimension=2, tiled=True)
    return (row_grad[None], up_sum, down_sum, pred_sum)


def solution(mesh):
    return jax.shard_map(
        on_device,
        mesh=mesh,
        in_specs=(
            P("joint", "section", None),
            P(None, "section"),
            P("section", None),
            P(),
            P("joint", None),
            P(),
            P(),
            P(),
            P(),
            P(),
            P(),
            P(),
            P(),
        ),
        out_specs=(
            P("joint", "section", None),
            P("joint", "section"),
            P("section", "joint"),
            P("joint", None, "section"),
        ),
        check_vma=False,
    )
```

profile of v0, /device:TPU:2, one launch (start us, length us, event | category | flops | bytes accessed | tf_op | source)
XLA Modules:
  0.0 2108.2 jit_solution(6235568972007815648)
XLA Ops:
  12.7 48.0 %all-gather.3.cloned.1.call-done = bf16[1024,1536]{1,0:T(8,128)(2,1)} async-done(((bf16[128,1536]{1,0:T(8,128)(2,1)}), bf16[1024,1536]{1,0:T(8,128)(2,1)}) %all-gather.3.cloned.1.call-update) | async-done | bytes 3145744 | tf_op jit(solution)/shard_map/all_gather | solution.py:191
  86.9 57.3 %reduce-scatter.7.cloned.1.call-done = f32[128,1536]{1,0:T(8,128)} async-done(((f32[1024,1536]{1,0:T(8,128)}), f32[128,1536]{1,0:T(8,128)}) %reduce-scatter.7.cloned.1.call-update) | async-done | bytes 786448 | tf_op jit(solution)/shard_map/reduce_scatter | solution.py:194
  233.3 6.8 broadcast_in_dim.223
  247.3 9.4 exponential_reduce_fusion.3
  256.7 9.8 reshape.609
  267.6 5.5 gather_fusion.31
  275.9 308.2 %while.74 = (s32[]{:T(128)}, f32[4,4]{1,0:T(4,128)S(1)}, pred[128]{0:T(512)(128)(4,1)S(1)}, f32[128,4]{1,0:T(8,128)S(1)}, f32[128,3]{1,0:T(8,128)}, /*index=5*/s32[]{:T(128)}, f32[]{:T(128)}, f32[1]{0:T(128)}) while((s32[]{:T(128)}, f32[4,4]{1,0:T(4,128)S(1)}, pred[128]{0:T(512)(128)(4,1)S(1)}, f32[128,4]{1,0:T(8,128)S(1)}, ...), condition=%wide.region_12.13_spmd, body=%wide.region_8.0_spmd.sunk | while | flops 476 | bytes 1144 | solution.py:68
  584.1 39.9 %while.75 = (s32[]{:T(128)}, f32[4]{0:T(128)S(1)}, pred[]{:T(512)}, f32[4,4]{1,0:T(4,128)S(1)}, s32[]{:T(128)}) while((s32[]{:T(128)}, f32[4]{0:T(128)S(1)}, pred[]{:T(512)}, f32[4,4]{1,0:T(4,128)S(1)}, s32[]{:T(128)}) %tuple.157), condition=%wide.region_16.17_spmd.clone, body=%wide.region_13.16_spmd.clone.sunk | while | flops 110 | bytes 486 | solution.py:246
  617.3 5.4 collective-permute-start
  624.0 567.5 %while.78 = (s32[]{:T(128)}, f32[4]{0:T(128)S(1)}, f32[128,4,4]{2,1,0:T(4,128)}, pred[128,4]{1,0:T(8,128)(4,1)}, f32[128,4]{1,0:T(8,128)S(1)}, /*index=5*/pred[1...) while((s32[]{:T(128)}, f32[4]{0:T(128)S(1)}, ...), condition=%wide.region_21.22_spmd.clone.clone, body=%wide.region_17.21_spmd.clone.clone.sunk | while | flops 296 | bytes 5132 | solution.py:52
  1191.5 53.7 %while.76 = (s32[]{:T(128)}, f32[4]{0:T(128)S(1)}, pred[]{:T(512)}, f32[4,4]{1,0:T(4,128)S(1)}, s32[]{:T(128)}, /*index=5*/s32[]{:T(128)}) while((s32[]{:T(128)}, f32[4]{0:T(128)S(1)}, pred[]{:T(512)}, f32[4,4]{1,0:T(4,128)S(1)}, s32[]{:T(128)}, /*index=5*/s32[]{:T(128)}) %tuple.183), condition=%wide.region_25.26_spmd.clone, body=%wide.region_22.25_spmd.clone.sunk | while | flops 110 | bytes 498 | solution.py:252
  1193.0 5.6 collective-permute-done.1
  1200.7 5.6 collective-permute-done.1
  1208.5 5.6 collective-permute-done.1
  1216.3 5.6 collective-permute-done.1
  1224.1 5.4 collective-permute-done.1
  1239.1 5.4 collective-permute-done.1
  1248.4 484.2 %while.77 = (s32[]{:T(128)}, f32[4]{0:T(128)S(1)}, f32[128,4]{1,0:T(8,128)S(1)}, f32[128,3]{1,0:T(8,128)S(1)}, pred[128]{0:T(512)(128)(4,1)S(1)}, /*index=5*/pre...) while((s32[]{:T(128)}, f32[4]{0:T(128)S(1)}, ...), condition=%wide.region_33.34_spmd.clone, body=%wide.region_28.33_spmd.clone.sunk | while | flops 133 | bytes 553 | solution.py:52
  1732.9 12.4 fusion.31
  1844.3 48.2 %all-gather.5.cloned.1.call-done = bf16[1024,1536]{1,0:T(8,128)(2,1)} async-done(((bf16[128,1536]{1,0:T(8,128)(2,1)}), bf16[1024,1536]{1,0:T(8,128)(2,1)}) %all-gather.5.cloned.1.call-update) | async-done | bytes 3145744 | tf_op jit(solution)/shard_map/all_gather | solution.py:270
  1897.8 7.8 convolution_convert_fusion
  1905.7 25.1 %reduce-scatter.13.cloned.1.call-done = f32[80,4]{1,0:T(8,128)} async-done(((f32[640,4]{1,0:T(8,128)}), f32[80,4]{1,0:T(8,128)}) %reduce-scatter.13.cloned.1.call-update) | async-done | bytes 1296
  1932.2 82.1 %reduce-scatter.11.cloned.1.call-done = bf16[384,48]{0,1:T(8,128)(2,1)} async-done(((bf16[384,1536]{0,1:T(8,128)(2,1)}), bf16[384,48]{0,1:T(8,128)(2,1)}) %reduce-scatter.11.cloned.1.call-update) | async-done | bytes 36880 | tf_op jit(solution)/shard_map/reduce_scatter | solution.py:288
  2015.7 83.2 %reduce-scatter.9.cloned.1.call-done = bf16[48,384]{1,0:T(8,128)(2,1)} async-done(((bf16[1536,384]{1,0:T(8,128)(2,1)}), bf16[48,384]{1,0:T(8,128)(2,1)}) %reduce-scatter.9.cloned.1.call-update) | async-done | bytes 36880 | tf_op jit(solution)/shard_map/reduce_scatter | solution.py:285
  (4273 shorter events, 1608.1 us)
Async XLA Ops:
  8.0 52.7 %all-gather.3.cloned.1.call-start = ((), (), s32[]{:S(2)}) async-start(), calls=%async_computation.4 | async-start | bytes 3538944 | tf_op jit(solution)/shard_map/all_gather | solution.py:191
  12.6 131.5 %reduce-scatter.7.cloned.1.call-start = ((), (), s32[]{:S(2)}) async-start(), calls=%async_computation.5 | async-start | bytes 7077888 | tf_op jit(solution)/shard_map/reduce_scatter | solution.py:194
  70.2 171.2 %all-reduce.5.cloned.1.call-start = ((), (), s32[]{:S(2)}) async-start(), calls=%async_computation.10 | async-start | bytes 327680
  74.8 1817.7 %all-gather.5.cloned.1.call-start = ((), (), s32[]{:S(2)}) async-start(), calls=%async_computation.6 | async-start | bytes 3538944 | tf_op jit(solution)/shard_map/all_gather | solution.py:270
  149.0 7.0 collective-permute-start.3
  161.1 7.8 collective-permute-start.5
  169.8 7.0 collective-permute-start.6
  184.8 7.0 collective-permute-start.9
  191.9 6.9 collective-permute-start.10
  200.9 7.8 collective-permute-start.12
  214.3 7.3 collective-permute-start.14
  222.3 19.8 collective-permute-start.15
  1191.7 6.9 collective-permute-start.1
  1199.4 6.9 collective-permute-start.1
  1207.2 6.9 collective-permute-start.1
  1215.0 6.9 collective-permute-start.1
  1764.1 8.0 collective-permute-start.20
  1782.7 7.6 collective-permute-start.23
  1790.3 8.5 collective-permute-start.24
  1808.9 8.3 collective-permute-start.27
  1823.6 8.0 collective-permute-start.29
  1843.2 87.5 %reduce-scatter.13.cloned.1.call-start = ((), (), s32[]{:S(2)}) async-start(), calls=%async_computation.9 | async-start | bytes 368640
  1844.2 170.1 %reduce-scatter.11.cloned.1.call-start = ((), (), s32[]{:S(2)}) async-start(), calls=%async_computation.8 | async-start | bytes 1216512 | tf_op jit(solution)/shard_map/reduce_scatter | solution.py:288
  1897.8 201.1 %reduce-scatter.9.cloned.1.call-start = ((), (), s32[]{:S(2)}) async-start(), calls=%async_computation.7 | async-start | bytes 1216512 | tf_op jit(solution)/shard_map/reduce_scatter | solution.py:285
  (55 other events, 2141.4 us)
Sparse Core Ops, SparseCore 0:
  12.8 47.9 all-gather.2
  70.3 73.7 reduce-scatter.6
  1843.3 49.0 all-gather.4
  1894.8 35.8 reduce-scatter.12
  1934.4 79.7 reduce-scatter.10
  2018.0 80.8 reduce-scatter.8
Sparse Core Ops, SparseCore 1:
  74.9 108.0 all-reduce.4
where the time goes:
time: 2140 us; the launch traced here: 2110 us
  other arithmetic  814 us (38%)
  local copies, waits for them, and re-layouts  667 us (31%)
  waiting for transfers between devices  429 us (20%)
  starting transfers between devices  85.7 us (4%)
  between operations  60.3 us (3%)
  matrix products  46.8 us (2%)
    dynamic_slice x384, local copies, waits for them, and re-layouts, block_matrix(): lax.scan(block_one_frame, identity_map, (blank_score, label_score, active))  219 us
    another operation x386, local copies, waits for them, and re-layouts  187 us
    dynamic_update_slice x512, local copies, waits for them, and re-layouts, run_block(): lax.scan(run_one_frame, vector, (blank_score, label_score, active))[0]  173 us
    broadcast_in_dim x130, other arithmetic, run_block(): lax.scan(run_one_frame, vector, (blank_score, label_score, active))[0]  171 us
    reduce_sum x128, other arithmetic, lower_paths(): partial_sums[:, None] - partial_sums[None, :]  112 us
    dynamic_update_slice x128, other arithmetic, run_block(): lax.scan(run_one_frame, vector, (blank_score, label_score, active))[0]  84.6 us
    add_any x128, other arithmetic, advance(): vector[None, :]  84.1 us
    reduce_scatter x1, waiting for transfers between devices, on_device(): lax.psum_scatter(up_part.astype(jnp.bfloat16), 'joint', scatter_dimension...  83.2 us

commit v1 on v0

--- a/solution.py
+++ b/solution.py
@@ -74,6 +74,79 @@
 
 def log_apply_back(transfer, vector):
     return jax.nn.logsumexp(transfer + vector[:, None], axis=0)
+
+
+def log_combine(earlier, later):
+    terms = later[..., :, :, None] + earlier[..., None, :, :]
+    return jax.nn.logsumexp(terms, axis=-2)
+
+
+def prefix_products(mats):
+    count = mats.shape[-3]
+    index = lax.broadcasted_iota(jnp.int32, (count, 1, 1), 0)
+    step = 1
+    while step < count:
+        shifted = jnp.concatenate([mats[..., :step, :, :], mats[..., :-step, :, :]], axis=-3)
+        mats = jnp.where(index >= step, log_combine(shifted, mats), mats)
+        step *= 2
+    return mats
+
+
+def both_products(mats):
+    backward = jnp.swapaxes(jnp.flip(mats, axis=0), -1, -2)
+    scanned = prefix_products(jnp.stack([mats, backward]))
+    return scanned[0], jnp.flip(scanned[1], axis=0)
+
+
+def identity_of(places):
+    row_ids = lax.broadcasted_iota(jnp.int32, (places, places), 0)
+    col_ids = lax.broadcasted_iota(jnp.int32, (places, places), 1)
+    return jnp.where(row_ids == col_ids, 0.0, NEG_BIG)
+
+
+def frame_matrices(blank_score, label_score, active):
+    frames, places = blank_score.shape
+    partial = jnp.concatenate(
+        [jnp.zeros((frames, 1), jnp.float32), jnp.cumsum(label_score, axis=1)], axis=1
+    )
+    row_ids = lax.broadcasted_iota(jnp.int32, (1, places, places), 1)
+    col_ids = lax.broadcasted_iota(jnp.int32, (1, places, places), 2)
+    moved = jnp.where(
+        col_ids <= row_ids,
+        blank_score[:, :, None] + partial[:, :, None] - partial[:, None, :],
+        NEG_BIG,
+    )
+    return jnp.where(active[:, None, None], moved, identity_of(places)[None])
+
+
+def ends_of(transfers, block_id, start_vec, finish_vec):
+    places = start_vec.shape[0]
+    forward, backward_t = both_products(transfers)
+    eye = identity_of(places)[None]
+    before = jnp.concatenate([eye, forward[:-1]], axis=0)[block_id]
+    after_t = jnp.concatenate([backward_t[1:], eye], axis=0)[block_id]
+    incoming = jax.nn.logsumexp(before + start_vec[None, :], axis=1)
+    leaving = jax.nn.logsumexp(after_t + finish_vec[None, :], axis=1)
+    return incoming, leaving
+
+
+def frame_grads(mats, forward, backward_t, incoming, leaving, active):
+    places = mats.shape[-1]
+    reached = jax.nn.logsumexp(forward + incoming[None, None, :], axis=2)
+    alpha = jnp.concatenate([incoming[None], reached[:-1]], axis=0)
+    remaining = jax.nn.logsumexp(backward_t + leaving[None, None, :], axis=2)
+    beta = jnp.concatenate([remaining[1:], leaving[None]], axis=0)
+    joint = alpha[:, None, :] + mats + beta[:, :, None]
+    frames = joint.shape[0]
+    flat = jax.nn.softmax(joint.reshape(frames, places * places), axis=1)
+    weights = jnp.where(active[:, None, None], flat.reshape(frames, places, places), 0.0)
+    blank_grad = -jnp.sum(weights, axis=2)
+    slot = lax.broadcasted_iota(jnp.int32, (places - 1, places, places), 0)
+    row_ids = lax.broadcasted_iota(jnp.int32, (places - 1, places, places), 1)
+    col_ids = lax.broadcasted_iota(jnp.int32, (places - 1, places, places), 2)
+    cover = ((col_ids <= slot) & (slot < row_ids)).astype(jnp.float32)
+    label_grad = -jnp.einsum("tkj,ikj->ti", weights, cover, precision=lax.Precision.HIGHEST)
+    return blank_grad, label_grad
 
 
 def joint_forward(frame_part, pred_here, label_row_ids, output_proj, output_bias):
@@ -234,29 +307,14 @@
     )
     frame_ids = section_id * block_len + jnp.arange(block_len, dtype=jnp.int32)
     active = frame_ids < frames_used
-    transfer = block_matrix(blank_score, label_score, active)
+    mats = frame_matrices(blank_score, label_score, active)
+    forward, backward_t = both_products(mats)
+    transfers = lax.all_gather(forward[-1], "section", axis=0, tiled=False)
     place_iota = jnp.arange(places, dtype=jnp.int32)
     start_vec = jnp.where(place_iota == 0, 0.0, NEG_BIG)
     finish_vec = jnp.where(place_iota == labels_used, 0.0, NEG_BIG)
-
-    def forward_turn(turn_index, carried):
-        passed = from_behind(log_apply(transfer, carried), "section", 1)
-        return jnp.where(section_id == 0, start_vec, passed)
-
-    incoming = lax.fori_loop(0, section_count - 1, forward_turn, start_vec)
-
-    def backward_turn(turn_index, carried):
-        passed = from_behind(log_apply_back(transfer, carried), "section", -1)
-        return jnp.where(section_id == section_count - 1, finish_vec, passed)
-
-    leaving = lax.fori_loop(0, section_count - 1, backward_turn, finish_vec)
-
-    def block_out(blank_in, label_in):
-        return run_block(incoming, blank_in, label_in, active)
-
-    end_alpha, pullback = jax.vjp(block_out, blank_score, label_score)
-    logprob = jax.nn.logsumexp(end_alpha + leaving)
-    blank_grad, label_grad = pullback(-jnp.exp(end_alpha + leaving - logprob))
+    incoming, leaving = ends_of(transfers, section_id, start_vec, finish_vec)
+    blank_grad, label_grad = frame_grads(mats, forward, backward_t, incoming, leaving, active)
     frame_part_grad, pred_part = joint_backward(
         blank_grad, label_grad, label_here, joined, posterior, output_proj
     )

time: 2140 us -> 688 us (0.32)
  other arithmetic: 814 us -> 42.8 us
  local copies, waits for them, and re-layouts: 667 us -> 88.2 us
  waiting for transfers between devices: 429 us -> 377 us
  starting transfers between devices: 85.7 us -> 42.2 us
  blocking collectives: 0 us -> 21.5 us
    dynamic_slice x384 -> x0, local copies, waits for them, and re-layouts: 219 us -> none  [block_matrix(): lax.scan(block_one_frame, identity_map, (blank_score, label_score, active))]
    another operation x386 -> x0, local copies, waits for them, and re-layouts: 187 us -> none
    dynamic_update_slice x512 -> x0, local copies, waits for them, and re-layouts: 173 us -> none  [run_block(): lax.scan(run_one_frame, vector, (blank_score, label_score, active))[0]]
    broadcast_in_dim x130 -> x0, other arithmetic: 171 us -> none  [run_block(): lax.scan(run_one_frame, vector, (blank_score, label_score, active))[0]]
    reduce_sum x399 -> x16, other arithmetic: 151 us -> 1.2 us  [the longest x10 0.44 us: log_combine(): return jax.nn.logsumexp(terms, axis=-2)]
    select_n x541 -> x28, other arithmetic: 94.8 us -> 6.06 us  [the longest x10 4.08 us: prefix_products(): mats = jnp.where(index >= step, log_combine(shifted, mats), mats)]
    dynamic_update_slice x128 -> x0, other arithmetic: 84.6 us -> none  [run_block(): lax.scan(run_one_frame, vector, (blank_score, label_score, active))[0]]
    add_any x128 -> x0, other arithmetic: 84.1 us -> none  [advance(): vector[None, :]]
where the time goes in v1:
time: 688 us; the launch traced here: 677 us
  waiting for transfers between devices  377 us (55%)
  local copies, waits for them, and re-layouts  88.2 us (13%)
  between operations  58.4 us (8%)
  matrix products  47 us (7%)
  other arithmetic  42.8 us (6%)
  starting transfers between devices  42.2 us (6%)
  blocking collectives  21.5 us (3%)
    reduce_scatter x1, waiting for transfers between devices, on_device(): lax.psum_scatter(up_part.astype(jnp.bfloat16), 'joint', scatter_dimension...  83.2 us
    reduce_scatter x1, waiting for transfers between devices, on_device(): lax.psum_scatter(down_part.astype(jnp.bfloat16), 'joint', scatter_dimensi...  82.1 us
    reduce_scatter x1, waiting for transfers between devices, on_device(): lax.psum_scatter(0.5 * jnp.dot(hidden, down_weight, preferred_element_typ...  52 us
    all_gather x1, waiting for transfers between devices, on_device(): gathered = lax.all_gather(normed_in, 'section', axis=0, tiled=True)  48 us
    ppermute x30, waiting for transfers between devices, partner_2(): return lax.ppermute(block, axis, route)  44.8 us
    ppermute x30, starting transfers between devices, partner_2(): return lax.ppermute(block, axis, route)  41.6 us
    all_gather x1, waiting for transfers between devices, on_device(): grad_all = lax.all_gather(row_grad, 'section', axis=0, tiled=True)  41.5 us
    unnamed x9, waiting for transfers between devices  25 us
  transfers between devices with their start and end apart: 37, of which 26 were waited for; matrix products, arithmetic and copies ran while one was open for 14% of the time, Pallas kernels for 0%

profile of v1, /device:TPU:2, one launch (start us, length us, event | category | flops | bytes accessed | tf_op | source)
XLA Modules:
  0.0 676.7 jit_solution(3359517512181103846)
XLA Ops:
  12.7 48.0 %all-gather.4.cloned.1.call-done = bf16[1024,1536]{1,0:T(8,128)(2,1)} async-done(((bf16[128,1536]{1,0:T(8,128)(2,1)}), bf16[1024,1536]{1,0:T(8,128)(2,1)}) %all-gather.4.cloned.1.call-update) | async-done | bytes 3145744 | tf_op jit(solution)/shard_map/all_gather | solution.py:264
  60.7 3.8 fusion.103
  65.7 4.5 convolution_multiply_fusion
  92.2 52.0 %reduce-scatter.7.cloned.1.call-done = f32[128,1536]{1,0:T(8,128)} async-done(((f32[1024,1536]{1,0:T(8,128)}), f32[128,1536]{1,0:T(8,128)}) %reduce-scatter.7.cloned.1.call-update) | async-done | bytes 786448 | tf_op jit(solution)/shard_map/reduce_scatter | solution.py:267
  149.7 5.6 collective-permute-done.1
  162.6 5.5 collective-permute-done.3
  200.2 3.1 collective-permute-start.10
  232.1 4.2 broadcast_in_dim.340
  236.3 6.8 %broadcast_in_dim.341 = pred[512,4096]{1,0:T(32,128)(4,1)} reshape(pred[128,4,4096]{2,1,0:T(4,128)(4,1)} %broadcast_in_dim.340) | data formatting | bytes 4194304 | tf_op jit(solution)/shard_map/jit(_where)/broadcast_in_dim | solution.py:184
  250.1 9.4 %exponential_reduce_fusion = (f32[512]{0:T(512)S(1)}, f32[512,4096]{1,0:T(8,128)}) fusion(f32[4096]{0:T(1024)S(1)} %copy-done.43, bf16[512,640]{1,0:T(8,128)(2,1)} %convert_element_type.82, bf16[640,4096]{1,0:T(8,128)(2,1)} %param.20), kind=kOutput, calls=%fused_computation.34 | convolution fusion | flops 2688548352 | bytes 14305280 | tf_op jit(solution)/shard_map/dot_general | solution.py:158
  259.6 9.8 %reshape.883 = f32[128,4,4096]{2,1,0:T(4,128)} reshape(f32[512,4096]{1,0:T(8,128)} %get-tuple-element.25) | data formatting | bytes 16777216 | tf_op jit(solution)/shard_map/reshape | solution.py:165
  270.4 5.5 gather_fusion.31
  283.1 21.5 %all-gather = f32[8,1,4,4]{3,2,1,0:T(4,128)S(1)} all-gather(f32[1,1,4,4]{3,2,1,0:T(4,128)S(1)} %copy.152), channel_id=2, replica_groups=mesh['section'=8,'joint'=32] {'section'}, dimensions={0}, use_global_device_ids=true | all-gather | bytes 576 | tf_op jit(solution)/shard_map/all_gather | solution.py:312
  308.6 12.4 %fusion.2 = f32[512,640]{1,0:T(8,128)} fusion(bf16[640,4096]{1,0:T(8,128)(2,1)} %param.20, pred[512,4096]{1,0:T(32,128)(4,1)} %broadcast_in_dim.341, f32[512,4096]{1,0:T(8,128)} %get-tuple-element.25, f32[512]{0:T(512)S(1)} %broadcast_in_dim.342, f32[512]{0:T(512)S(1)} %neg.26, f32[512]{0:T(512)S(1)} %mul.130, f32[512]{0:T(512)S(1)} %get-tuple-element.24, ...), kind=kOutput, calls=%fused_computation.44 | convolution fusion | flops 2702442496 | bytes 17707008 | tf_op jit(solution)/shard_map/dot_general | solution.py:187
  345.2 2.7 collective-permute-done.18
  365.7 4.7 collective-permute-start.22
  388.7 4.2 collective-permute-done.25
  399.2 4.6 collective-permute-start.27
  419.5 41.5 %all-gather.6.cloned.1.call-done = bf16[1024,1536]{1,0:T(8,128)(2,1)} async-done(((bf16[128,1536]{1,0:T(8,128)(2,1)}), bf16[1024,1536]{1,0:T(8,128)(2,1)}) %all-gather.6.cloned.1.call-update) | async-done | bytes 3145744 | tf_op jit(solution)/shard_map/all_gather | solution.py:328
  461.0 5.3 fusion.1
  466.6 7.8 %convolution_convert_fusion = bf16[1536,384]{1,0:T(8,128)(2,1)} fusion(bf16[1024,1536]{1,0:T(8,128)(2,1)} %all-gather.4.cloned.1.call-done, f32[1024,384]{1,0:T(8,128)} %copy-done.47, bf16[1024,1536]{1,0:T(8,128)(2,1)} %all-gather.6.cloned.1.call-done, bf16[384,1536]{1,0:T(8,128)(2,1)S(1)} %copy-done.42), kind=kOutput, calls=%fused_computation.40 | convolution fusion | flops 2420441088 | bytes 10223616 | tf_op jit(solution)/shard_map/dot_general | solution.py:336
  474.5 24.8 %reduce-scatter.13.cloned.1.call-done = f32[80,4]{1,0:T(8,128)} async-done(((f32[640,4]{1,0:T(8,128)}), f32[80,4]{1,0:T(8,128)}) %reduce-scatter.13.cloned.1.call-update) | async-done | bytes 1296
  500.7 82.1 %reduce-scatter.11.cloned.1.call-done = bf16[384,48]{0,1:T(8,128)(2,1)} async-done(((bf16[384,1536]{0,1:T(8,128)(2,1)}), bf16[384,48]{0,1:T(8,128)(2,1)}) %reduce-scatter.11.cloned.1.call-update) | async-done | bytes 36880 | tf_op jit(solution)/shard_map/reduce_scatter | solution.py:346
  584.2 83.2 %reduce-scatter.9.cloned.1.call-done = bf16[48,384]{1,0:T(8,128)(2,1)} async-done(((bf16[1536,384]{1,0:T(8,128)(2,1)}), bf16[48,384]{1,0:T(8,128)(2,1)}) %reduce-scatter.9.cloned.1.call-update) | async-done | bytes 36880 | tf_op jit(solution)/shard_map/reduce_scatter | solution.py:343
  (477 shorter events, 165.2 us)
Async XLA Ops:
  8.0 52.7 %all-gather.4.cloned.1.call-start = ((), (), s32[]{:S(2)}) async-start(), calls=%async_computation.4 | async-start | bytes 3538944 | tf_op jit(solution)/shard_map/all_gather | solution.py:264
  12.6 131.5 %reduce-scatter.7.cloned.1.call-start = ((), (), s32[]{:S(2)}) async-start(), calls=%async_computation.5 | async-start | bytes 7077888 | tf_op jit(solution)/shard_map/reduce_scatter | solution.py:267
  70.2 174.2 %all-reduce.6.cloned.1.call-start = ((), (), s32[]{:S(2)}) async-start(), calls=%async_computation.10 | async-start | bytes 327680
  74.8 386.2 %all-gather.6.cloned.1.call-start = ((), (), s32[]{:S(2)}) async-start(), calls=%async_computation.6 | async-start | bytes 3538944 | tf_op jit(solution)/shard_map/all_gather | solution.py:328
  149.0 6.3 collective-permute-start.1
  159.8 8.3 %collective-permute-start.3 = (bf16[128,640]{1,0:T(8,128)(2,1)S(1)}, bf16[128,640]{1,0:T(8,128)(2,1)S(1)}, u32[]{:S(2)}, u32[]{:S(2)}) collective-permute-start(bf16[128,640]{1,0:T(8,128)(2,1)S(1)} %broadcast_select_fusion.2), channel_id=1, source_target_pairs={{0,4},{4,0},{1,5},{5,1},{2,6},{6,2},{3,7},{7,3},{8,12},{12,8},{9,1... | collective-permute-start | bytes 491528 | tf_op jit(solution)/shard_map/ppermute | solution.py:16
  177.1 6.8 collective-permute-start.6
  183.8 7.3 %collective-permute-start.7 = (bf16[128,640]{1,0:T(8,128)(2,1)S(1)}, bf16[128,640]{1,0:T(8,128)(2,1)S(1)}, u32[]{:S(2)}, u32[]{:S(2)}) collective-permute-start(bf16[128,640]{1,0:T(8,128)(2,1)S(1)} %broadcast_select_fusion.6), channel_id=1, source_target_pairs={{0,4},{4,0},{1,5},{5,1},{2,6},{6,2},{3,7},{7,3},{8,12},{12,8},{9,1... | collective-permute-start | bytes 491528 | tf_op jit(solution)/shard_map/ppermute | solution.py:16
  191.2 5.9 collective-permute-start.8
  200.2 8.2 %collective-permute-start.10 = (bf16[128,640]{1,0:T(8,128)(2,1)S(1)}, bf16[128,640]{1,0:T(8,128)(2,1)S(1)}, u32[]{:S(2)}, u32[]{:S(2)}) collective-permute-start(bf16[128,640]{1,0:T(8,128)(2,1)S(1)} %broadcast_select_fusion.9), channel_id=1, source_target_pairs={{0,16},{16,0},{1,17},{17,1},{2,18},{18,2},{3,19},{19,3},{4,20},{20... | collective-permute-start | bytes 491528 | tf_op jit(solution)/shard_map/ppermute | solution.py:16
  208.5 5.8 collective-permute-start.11
  214.3 6.9 %collective-permute-start.12 = (bf16[128,640]{1,0:T(8,128)(2,1)S(1)}, bf16[128,640]{1,0:T(8,128)(2,1)S(1)}, u32[]{:S(2)}, u32[]{:S(2)}) collective-permute-start(bf16[128,640]{1,0:T(8,128)(2,1)S(1)} %broadcast_select_fusion.11), channel_id=1, source_target_pairs={{0,4},{4,0},{1,5},{5,1},{2,6},{6,2},{3,7},{7,3},{8,12},{12,8},{9,1... | collective-permute-start | bytes 491528 | tf_op jit(solution)/shard_map/ppermute | solution.py:16
  221.9 23.2 %collective-permute-start.13 = (bf16[128,640]{1,0:T(8,128)(2,1)S(1)}, bf16[128,640]{1,0:T(8,128)(2,1)S(1)}, u32[]{:S(2)}, u32[]{:S(2)}) collective-permute-start(bf16[128,640]{1,0:T(8,128)(2,1)S(1)} %broadcast_select_fusion.12), channel_id=1, source_target_pairs={{0,2},{2,0},{1,3},{3,1},{4,6},{6,4},{5,7},{7,5},{8,10},{10,8},{9,1... | collective-permute-start | bytes 491528 | tf_op jit(solution)/shard_map/ppermute | solution.py:16
  328.6 6.9 %collective-permute-start.16 = (bf16[128,640]{1,0:T(8,128)(2,1)S(1)}, bf16[128,640]{1,0:T(8,128)(2,1)}, u32[]{:S(2)}, u32[]{:S(2)}) collective-permute-start(bf16[128,640]{1,0:T(8,128)(2,1)S(1)} %broadcast_select_fusion.14), channel_id=1, source_target_pairs={{0,2},{2,0},{1,3},{3,1},{4,6},{6,4},{5,7},{7,5},{8,10},{10,8},{9,1... | collective-permute-start | bytes 491528 | tf_op jit(solution)/shard_map/ppermute | solution.py:16
  340.1 7.8 %collective-permute-start.18 = (bf16[128,640]{1,0:T(8,128)(2,1)S(1)}, bf16[128,640]{1,0:T(8,128)(2,1)}, u32[]{:S(2)}, u32[]{:S(2)}) collective-permute-start(bf16[128,640]{1,0:T(8,128)(2,1)S(1)} %broadcast_select_fusion.16), channel_id=1, source_target_pairs={{0,4},{4,0},{1,5},{5,1},{2,6},{6,2},{3,7},{7,3},{8,12},{12,8},{9,1... | collective-permute-start | bytes 491528 | tf_op jit(solution)/shard_map/ppermute | solution.py:16
  358.4 7.3 %collective-permute-start.21 = (bf16[128,640]{1,0:T(8,128)(2,1)S(1)}, bf16[128,640]{1,0:T(8,128)(2,1)}, u32[]{:S(2)}, u32[]{:S(2)}) collective-permute-start(bf16[128,640]{1,0:T(8,128)(2,1)S(1)} %broadcast_select_fusion.19), channel_id=1, source_target_pairs={{0,8},{8,0},{1,9},{9,1},{2,10},{10,2},{3,11},{11,3},{4,12},{12,4},... | collective-permute-start | bytes 491528 | tf_op jit(solution)/shard_map/ppermute | solution.py:16
  365.7 8.8 %collective-permute-start.22 = (bf16[128,640]{1,0:T(8,128)(2,1)S(1)}, bf16[128,640]{1,0:T(8,128)(2,1)}, u32[]{:S(2)}, u32[]{:S(2)}) collective-permute-start(bf16[128,640]{1,0:T(8,128)(2,1)S(1)} %broadcast_select_fusion.20), channel_id=1, source_target_pairs={{0,4},{4,0},{1,5},{5,1},{2,6},{6,2},{3,7},{7,3},{8,12},{12,8},{9,1... | collective-permute-start | bytes 491528 | tf_op jit(solution)/shard_map/ppermute | solution.py:16
  374.6 6.3 collective-permute-start.23
  384.6 8.3 %collective-permute-start.25 = (bf16[128,640]{1,0:T(8,128)(2,1)S(1)}, bf16[128,640]{1,0:T(8,128)(2,1)}, u32[]{:S(2)}, u32[]{:S(2)}) collective-permute-start(bf16[128,640]{1,0:T(8,128)(2,1)S(1)} %broadcast_select_fusion.23), channel_id=1, source_target_pairs={{0,16},{16,0},{1,17},{17,1},{2,18},{18,2},{3,19},{19,3},{4,20},{20... | collective-permute-start | bytes 491528 | tf_op jit(solution)/shard_map/ppermute | solution.py:16
  393.0 6.2 collective-permute-start.26
  399.2 8.0 %collective-permute-start.27 = (bf16[128,640]{1,0:T(8,128)(2,1)S(1)}, bf16[128,640]{1,0:T(8,128)(2,1)}, u32[]{:S(2)}, u32[]{:S(2)}) collective-permute-start(bf16[128,640]{1,0:T(8,128)(2,1)S(1)} %broadcast_select_fusion.25), channel_id=1, source_target_pairs={{0,4},{4,0},{1,5},{5,1},{2,6},{6,2},{3,7},{7,3},{8,12},{12,8},{9,1... | collective-permute-start | bytes 491528 | tf_op jit(solution)/shard_map/ppermute | solution.py:16
  418.5 80.8 %reduce-scatter.13.cloned.1.call-start = ((), (), s32[]{:S(2)}) async-start(), calls=%async_computation.9 | async-start | bytes 368640
  419.5 163.3 %reduce-scatter.11.cloned.1.call-start = ((), (), s32[]{:S(2)}) async-start(), calls=%async_computation.8 | async-start | bytes 1216512 | tf_op jit(solution)/shard_map/reduce_scatter | solution.py:346
  466.3 201.1 %reduce-scatter.9.cloned.1.call-start = ((), (), s32[]{:S(2)}) async-start(), calls=%async_computation.7 | async-start | bytes 1216512 | tf_op jit(solution)/shard_map/reduce_scatter | solution.py:343
  (61 other events, 1118.0 us)
Sparse Core Ops, SparseCore 0:
  12.8 47.9 all-gather.3
  70.4 73.7 reduce-scatter.6
  418.6 42.3 all-gather.5
  463.4 35.8 reduce-scatter.12
  503.0 79.7 reduce-scatter.10
  586.5 80.8 reduce-scatter.8
Sparse Core Ops, SparseCore 1:
  74.9 107.8 all-reduce.5

commit v2 on v1

--- a/solution.py
+++ b/solution.py
@@ -235,6 +235,15 @@
         other = partner_2(payload, "joint", stride.bit_length() - 1)
         payload = jnp.where(takes, other, payload)
     return payload
+
+
+def route_rows(payload, source_of, axis):
+    count = lax.axis_size(axis)
+    rows = payload.shape[0]
+    spread = lax.all_to_all(payload, axis, 0, 0, tiled=True)
+    spread = spread.reshape(count, rows // count, *payload.shape[1:])
+    picked = jnp.take(spread, source_of, axis=0).reshape(payload.shape)
+    return lax.all_to_all(picked, axis, 0, 0, tiled=True)
 
 
 def on_device(
@@ -277,7 +286,7 @@
     order_iota = jnp.arange(utterances, dtype=jnp.int32)
     inverse = jnp.zeros((utterances,), jnp.int32).at[owner_index].set(order_iota)
     own_utterance = inverse[joint_id]
-    owner_frames = route_owner(frame_part, owner_index, joint_id, joint_count)
+    owner_frames = route_rows(frame_part, inverse, "joint")
     context = jnp.concatenate([jnp.zeros((utterances, 1), jnp.int32), label_ids], axis=1)
     vocab_rows = embedding.shape[0]
     vocab_ids = joint_id * vocab_rows + jnp.arange(vocab_rows, dtype=jnp.int32)
@@ -318,7 +327,7 @@
     frame_part_grad, pred_part = joint_backward(
         blank_grad, label_grad, label_here, joined, posterior, output_proj
     )
-    part_grad = route_holder(frame_part_grad, inverse, joint_id, joint_count)
+    part_grad = route_rows(frame_part_grad, owner_index, "joint")
     unit_grad = lax.dot_general(
         part_grad, encoder_proj, (((1,), (1,)), ((), ())), preferred_element_type=jnp.float32
     )
@@ -339,14 +348,13 @@
     down_part = 0.5 * lax.dot_general(
         hidden, grad_all, (((0,), (0,)), ((), ())), preferred_element_type=jnp.float32
     )
-    up_sum, down_sum = (
-        lax.psum_scatter(
-            up_part.astype(jnp.bfloat16), "joint", scatter_dimension=0, tiled=True
-        ).astype(jnp.float32),
-        lax.psum_scatter(
-            down_part.astype(jnp.bfloat16), "joint", scatter_dimension=1, tiled=True
-        ).astype(jnp.float32),
-    )
+    weight_parts = jnp.concatenate([up_part, down_part.T], axis=1).astype(jnp.bfloat16)
+    weight_sums = lax.psum_scatter(weight_parts, "joint", scatter_dimension=0, tiled=True).astype(
+        jnp.float32
+    )
+    hidden_here = up_part.shape[1]
+    up_sum = weight_sums[:, :hidden_here]
+    down_sum = weight_sums[:, hidden_here:].T
     pred_sum = lax.psum_scatter(pred_part[None], "section", scatter_dimension=2, tiled=True)
     return (row_grad[None], up_sum, down_sum, pred_sum)
 

time: 688 us -> 491 us (0.71); the launches traced: 677 us -> 489 us
  waiting for transfers between devices: 377 us -> 282 us
  between operations: 58.4 us -> 18.7 us
  local copies, waits for them, and re-layouts: 88.2 us -> 53.1 us
  starting transfers between devices: 42.2 us -> 19.7 us
  blocking collectives: 21.5 us -> 35.9 us
  other arithmetic: 42.8 us -> 35.1 us
    reduce_scatter x2 -> x0, waiting for transfers between devices: 165 us -> none  [the longest x1 83.2 us: on_device(): lax.psum_scatter(up_part.astype(jnp.bfloat16), 'joint', scatter_dimension...]
    unnamed x9, waiting for transfers between devices: 25 us -> 123 us
    ppermute x30 -> x0, waiting for transfers between devices: 44.8 us -> none  [partner_2(): return lax.ppermute(block, axis, route)]
    ppermute x30 -> x0, starting transfers between devices: 41.6 us -> none  [partner_2(): return lax.ppermute(block, axis, route)]
    gather x30 -> x2, local copies, waits for them, and re-layouts: 21.7 us -> 1.43 us  [route_rows(): picked = jnp.take(spread, source_of, axis=0).reshape(payload.shape)]
    all_to_all x0 -> x3, starting transfers between devices: none -> 19.2 us  [the longest x2 12.4 us: route_rows(): spread = lax.all_to_all(payload, axis, 0, 0, tiled=True)]
    dynamic_slice x32 -> x1, local copies, waits for them, and re-layouts: 19.6 us -> 0.59 us  [on_device(): own_utterance = inverse[joint_id]]
    all_to_all x0 -> x3, waiting for transfers between devices: none -> 12.3 us  [the longest x2 6.84 us: route_rows(): spread = lax.all_to_all(payload, axis, 0, 0, tiled=True)]
  transfers between devices with their start and end apart: 37 -> 9, of which waited for: 26 -> 8; matrix products, arithmetic and copies ran while one was open for 14% -> 10% of each run, Pallas kernels for 0% -> 0%
where the time goes in v2:
time: 491 us; the launch traced here: 489 us
  waiting for transfers between devices  282 us (57%)
  local copies, waits for them, and re-layouts  53.1 us (11%)
  matrix products  44.7 us (9%)
  blocking collectives  35.9 us (7%)
  other arithmetic  35.1 us (7%)
  starting transfers between devices  19.7 us (4%)
  between operations  18.7 us (4%)
    unnamed x9, waiting for transfers between devices  123 us
    reduce_scatter x1, waiting for transfers between devices, on_device(): lax.psum_scatter(0.5 * jnp.dot(hidden, down_weight, preferred_element_typ...  58.7 us
    all_gather x1, waiting for transfers between devices, on_device(): gathered = lax.all_gather(normed_in, 'section', axis=0, tiled=True)  48 us
    all_gather x1, waiting for transfers between devices, on_device(): grad_all = lax.all_gather(row_grad, 'section', axis=0, tiled=True)  39.6 us
    all_gather x1, blocking collectives, on_device(): transfers = lax.all_gather(forward[-1], 'section', axis=0, tiled=False)  24.3 us
    all_to_all x2, starting transfers between devices, route_rows(): spread = lax.all_to_all(payload, axis, 0, 0, tiled=True)  12.4 us
    dot_general x1, matrix products, joint_backward(): lax.dot_general(logit_grad, output_proj, (((1,), (1,)), ((), ())), prefer...  12.4 us
    unnamed x58, local copies, waits for them, and re-layouts  11.8 us
  transfers between devices with their start and end apart: 9, of which 8 were waited for; matrix products, arithmetic and copies ran while one was open for 10% of the time, Pallas kernels for 0%

profile of v2, /device:TPU:2, one launch (start us, length us, event | category | flops | bytes accessed | tf_op | source)
XLA Modules:
  0.0 489.2 jit_solution(5414345556971293496)
XLA Ops:
  12.7 48.0 %all-gather.4.cloned.1.call-done = bf16[1024,1536]{1,0:T(8,128)(2,1)} async-done(((bf16[128,1536]{1,0:T(8,128)(2,1)}), bf16[1024,1536]{1,0:T(8,128)(2,1)}) %all-gather.4.cloned.1.call-update) | async-done | bytes 3145744 | tf_op jit(solution)/shard_map/all_gather | solution.py:273
  60.7 4.0 fusion.83
  65.9 4.5 convolution_multiply_fusion
  85.7 58.7 %reduce-scatter.8.cloned.1.call-done = f32[128,1536]{1,0:T(8,128)} async-done(((f32[1024,1536]{1,0:T(8,128)}), f32[128,1536]{1,0:T(8,128)}) %reduce-scatter.8.cloned.1.call-update) | async-done | bytes 786448 | tf_op jit(solution)/shard_map/reduce_scatter | solution.py:276
  148.4 7.4 %all-to-all-start = ((bf16[32,4,640]{2,1,0:T(4,128)(2,1)}), bf16[32,4,640]{2,1,0:T(4,128)(2,1)S(1)}, u32[]{:S(2)}, u32[]{:S(2)}) async-start(bf16[32,4,640]{2,1,0:T(4,128)(2,1)} %all_to_all.20), calls=%async_computation.1 | async-start | bytes 327680 | tf_op jit(solution)/shard_map/all_to_all | solution.py:243
  157.0 3.5 broadcast_in_dim.319
  160.5 6.8 %broadcast_in_dim.320 = pred[512,4096]{1,0:T(32,128)(4,1)} reshape(pred[128,4,4096]{2,1,0:T(4,128)(4,1)} %broadcast_in_dim.319) | data formatting | bytes 4194304 | tf_op jit(solution)/shard_map/jit(_where)/broadcast_in_dim | solution.py:184
  168.5 13.8 %all-reduce.6.cloned.1.call-done = bf16[128,640]{1,0:T(8,128)(2,1)} async-done(((bf16[128,640]{1,0:T(8,128)(2,1)}), bf16[128,640]{1,0:T(8,128)(2,1)}) %all-reduce.6.cloned.1.call-update) | async-done | bytes 163856
  184.6 6.8 %all-to-all-start.1 = ((bf16[32,4,640]{2,1,0:T(4,128)(2,1)}), bf16[32,4,640]{2,1,0:T(4,128)(2,1)}, u32[]{:S(2)}, u32[]{:S(2)}) async-start(bf16[32,4,640]{2,1,0:T(4,128)(2,1)} %broadcast_select_fusion.1), calls=%async_computation.2 | async-start | bytes 327680 | tf_op jit(solution)/shard_map/all_to_all | solution.py:246
  192.9 5.5 %all-to-all-done.1 = bf16[32,4,640]{2,1,0:T(4,128)(2,1)} async-done(((bf16[32,4,640]{2,1,0:T(4,128)(2,1)}), bf16[32,4,640]{2,1,0:T(4,128)(2,1)}, u32[]{:S(2)}, u32[]{:S(2)}) %all-to-all-start.1) | async-done | bytes 163872 | tf_op jit(solution)/shard_map/all_to_all | solution.py:246
  202.7 9.4 %exponential_reduce_fusion = (f32[512]{0:T(512)S(1)}, f32[512,4096]{1,0:T(8,128)}) fusion(f32[4096]{0:T(1024)} %param.23, bf16[512,640]{1,0:T(8,128)(2,1)} %convert_element_type.86, bf16[640,4096]{1,0:T(8,128)(2,1)} %param.22), kind=kOutput, calls=%fused_computation.6 | convolution fusion | flops 2688548352 | bytes 14305280 | tf_op jit(solution)/shard_map/dot_general | solution.py:158
  212.1 9.8 %reshape.817 = f32[128,4,4096]{2,1,0:T(4,128)} reshape(f32[512,4096]{1,0:T(8,128)} %get-tuple-element.38) | data formatting | bytes 16777216 | tf_op jit(solution)/shard_map/reshape | solution.py:165
  222.9 5.5 %gather_fusion.1 = f32[384]{0:T(512)S(1)} fusion(f32[128,3,4096]{2,1,0:T(4,128)} %bitcast.117, s32[384]{0:T(512)S(1)} %reshape.846), kind=kCustom, calls=%fused_computation.3 | custom fusion | bytes 7680 | tf_op jit(solution)/shard_map/jit(take_along_axis)/gather | solution.py:171
  236.0 24.3 %all-gather = f32[8,1,4,4]{3,2,1,0:T(4,128)S(1)} all-gather(f32[1,1,4,4]{3,2,1,0:T(4,128)S(1)} %copy.158), channel_id=2, replica_groups=mesh['section'=8,'joint'=32] {'section'}, dimensions={0}, use_global_device_ids=true | all-gather | bytes 576 | tf_op jit(solution)/shard_map/all_gather | solution.py:321
  266.9 12.4 %fusion.2 = f32[512,640]{1,0:T(8,128)} fusion(bf16[640,4096]{1,0:T(8,128)(2,1)} %param.22, pred[512,4096]{1,0:T(32,128)(4,1)} %broadcast_in_dim.320, f32[512,4096]{1,0:T(8,128)} %get-tuple-element.38, f32[512]{0:T(512)S(1)} %broadcast_in_dim.321, f32[512]{0:T(512)S(1)} %neg.26, f32[512]{0:T(512)S(1)} %mul.131, f32[512]{0:T(512)S(1)} %get-tuple-element.37, ...), kind=kOutput, calls=%fused_computation.17 | convolution fusion | flops 2702442496 | bytes 17707008 | tf_op jit(solution)/shard_map/dot_general | solution.py:187
  284.9 4.9 %all-to-all-start.2 = ((bf16[32,4,640]{2,1,0:T(4,128)(2,1)}), bf16[32,4,640]{2,1,0:T(4,128)(2,1)S(1)}, u32[]{:S(2)}, u32[]{:S(2)}) async-start(bf16[32,4,640]{2,1,0:T(4,128)(2,1)} %convert_element_type.90), calls=%async_computation.3 | async-start | bytes 327680 | tf_op jit(solution)/shard_map/all_to_all | solution.py:243
  289.9 6.8 %all-to-all-done.2 = bf16[32,4,640]{2,1,0:T(4,128)(2,1)S(1)} async-done(((bf16[32,4,640]{2,1,0:T(4,128)(2,1)}), bf16[32,4,640]{2,1,0:T(4,128)(2,1)S(1)}, u32[]{:S(2)}, u32[]{:S(2)}) %all-to-all-start.2) | async-done | bytes 163872 | tf_op jit(solution)/shard_map/all_to_all | solution.py:243
  297.6 11.5 %all_to_all.30 = bf16[32,4,640]{2,1,0:T(4,128)(2,1)S(1)} all-to-all(bf16[32,4,640]{2,1,0:T(4,128)(2,1)S(1)} %broadcast_select_fusion), channel_id=1, replica_groups=mesh['section'=8,'joint'=32] {'joint'}, dimensions={0} | all-to-all | bytes 327680 | tf_op jit(solution)/shard_map/all_to_all | solution.py:246
  312.5 39.6 %all-gather.6.cloned.1.call-done = bf16[1024,1536]{1,0:T(8,128)(2,1)} async-done(((bf16[128,1536]{1,0:T(8,128)(2,1)}), bf16[1024,1536]{1,0:T(8,128)(2,1)}) %all-gather.6.cloned.1.call-update) | async-done | bytes 3145744 | tf_op jit(solution)/shard_map/all_gather | solution.py:337
  352.0 6.8 %convolution_convert_fusion = bf16[1536,384]{0,1:T(8,128)(2,1)S(1)} fusion(bf16[1024,1536]{1,0:T(8,128)(2,1)} %all-gather.4.cloned.1.call-done, f32[1024,384]{1,0:T(8,128)} %copy-done.22, bf16[1024,1536]{1,0:T(8,128)(2,1)} %all-gather.6.cloned.1.call-done, bf16[384,1536]{1,0:T(8,128)(2,1)} %param.17), kind=kOutput, calls=%fused_computation.12 | convolution fusion | flops 2420441088 | bytes 10223616 | tf_op jit(solution)/shard_map/dot_general | solution.py:345
  358.8 3.8 fusion.1
  364.2 4.3 copy.169
  368.5 21.8 %reduce-scatter.12.cloned.1.call-done = f32[80,4]{1,0:T(8,128)} async-done(((f32[640,4]{1,0:T(8,128)}), f32[80,4]{1,0:T(8,128)}) %reduce-scatter.12.cloned.1.call-update) | async-done | bytes 1296
  391.7 87.7 %reduce-scatter.10.cloned.1.call-done = bf16[48,768]{1,0:T(8,128)(2,1)} async-done(((bf16[1536,768]{1,0:T(8,128)(2,1)}), bf16[48,768]{1,0:T(8,128)(2,1)}) %reduce-scatter.10.cloned.1.call-update) | async-done | bytes 73744
  (261 shorter events, 62.8 us)
Async XLA Ops:
  8.0 139.1 %copy-start = (bf16[1536,640]{1,0:T(8,128)(2,1)S(1)}, bf16[1536,640]{1,0:T(8,128)(2,1)}, u32[]{:S(2)}) copy-start(bf16[1536,640]{1,0:T(8,128)(2,1)} %param.18) | copy-start | bytes 5898244
  8.0 52.7 %all-gather.4.cloned.1.call-start = ((), (), s32[]{:S(2)}) async-start(), calls=%async_computation.7 | async-start | bytes 3538944 | tf_op jit(solution)/shard_map/all_gather | solution.py:273
  12.6 53.3 %copy-start.16 = (bf16[384,1536]{1,0:T(8,128)(2,1)S(1)}, bf16[384,1536]{1,0:T(8,128)(2,1)}, u32[]{:S(2)}) copy-start(bf16[384,1536]{1,0:T(8,128)(2,1)} %param.17) | copy-start | bytes 3538948
  12.6 131.8 %reduce-scatter.8.cloned.1.call-start = ((), (), s32[]{:S(2)}) async-start(), calls=%async_computation.8 | async-start | bytes 7077888 | tf_op jit(solution)/shard_map/reduce_scatter | solution.py:276
  70.4 12.8 %copy-start.5 = (f32[2,640]{1,0:T(2,128)S(1)}, f32[2,640]{1,0:T(2,128)}, u32[]{:S(2)}) copy-start(f32[2,640]{1,0:T(2,128)} %param.20) | copy-start | bytes 15364
  70.4 12.8 %copy-start.17 = (s32[32]{0:T(128)S(1)}, s32[32]{0:T(128)}, u32[]{:S(2)}) copy-start(s32[32]{0:T(128)} %param.24) | copy-start | bytes 388
  70.4 13.4 %copy-start.18 = (s32[32]{0:T(128)S(1)}, s32[32]{0:T(128)}, u32[]{:S(2)}) copy-start(s32[32]{0:T(128)} %param.25) | copy-start | bytes 388
  70.4 73.9 %copy-start.1 = (bf16[1,128,1536]{2,1,0:T(8,128)(2,1)S(1)}, bf16[1,128,1536]{2,1,0:T(8,128)(2,1)}, u32[]{:S(2)}) copy-start(bf16[1,128,1536]{2,1,0:T(8,128)(2,1)} %param.15) | copy-start | bytes 1179652
  70.5 111.9 %all-reduce.6.cloned.1.call-start = ((), (), s32[]{:S(2)}) async-start(), calls=%async_computation.12 | async-start | bytes 327680
  76.3 69.4 %copy-start.7 = (s32[3]{0:T(128)}, s32[3]{0:T(128)S(1)}, u32[]{:S(2)}) copy-start(s32[3]{0:T(128)S(1)} %broadcast_add_fusion) | copy-start | bytes 40
  76.4 6.7 %copy-start.9 = (pred[3]{0:T(512)(128)(4,1)}, pred[3]{0:T(512)(128)(4,1)S(1)}, u32[]{:S(2)}) copy-start(pred[3]{0:T(512)(128)(4,1)S(1)} %broadcast_compare_fusion) | copy-start | bytes 13
  76.9 80.0 %copy-start.15 = (pred[4,4]{1,0:T(4,128)(4,1)}, pred[4,4]{1,0:T(4,128)(4,1)S(1)}, u32[]{:S(2)}) copy-start(pred[4,4]{1,0:T(4,128)(4,1)S(1)} %iota_compare_fusion.7) | copy-start | bytes 52
  148.4 34.7 %all-to-all-start = ((bf16[32,4,640]{2,1,0:T(4,128)(2,1)}), bf16[32,4,640]{2,1,0:T(4,128)(2,1)S(1)}, u32[]{:S(2)}, u32[]{:S(2)}) async-start(bf16[32,4,640]{2,1,0:T(4,128)(2,1)} %all_to_all.20), calls=%async_computation.1 | async-start | bytes 327680 | tf_op jit(solution)/shard_map/all_to_all | solution.py:243
  160.5 6.8 %copy-start.21 = (u32[256]{0:T(256)S(1)}, u32[256]{0:T(256)}, u32[]{:S(2)}) copy-start(u32[256]{0:T(256)} %constant.132) | copy-start | bytes 3076
  160.5 23.3 %copy-start.12 = (pred[32]{0:T(512)(128)(4,1)S(1)}, pred[32]{0:T(512)(128)(4,1)}, u32[]{:S(2)}) copy-start(pred[32]{0:T(512)(128)(4,1)} %compare_and_fusion.1) | copy-start | bytes 100
  184.6 13.7 %all-to-all-start.1 = ((bf16[32,4,640]{2,1,0:T(4,128)(2,1)}), bf16[32,4,640]{2,1,0:T(4,128)(2,1)}, u32[]{:S(2)}, u32[]{:S(2)}) async-start(bf16[32,4,640]{2,1,0:T(4,128)(2,1)} %broadcast_select_fusion.1), calls=%async_computation.2 | async-start | bytes 327680 | tf_op jit(solution)/shard_map/all_to_all | solution.py:246
  228.4 34.1 %copy-start.11 = (pred[8]{0:T(512)(128)(4,1)S(1)}, pred[8]{0:T(512)(128)(4,1)}, u32[]{:S(2)}) copy-start(pred[8]{0:T(512)(128)(4,1)} %iota_compare_fusion.17) | copy-start | bytes 28
  228.4 34.4 %copy-start.6 = (f32[4]{0:T(128)S(1)}, f32[4]{0:T(128)}, u32[]{:S(2)}) copy-start(f32[4]{0:T(128)} %compare_select_fusion.3) | copy-start | bytes 52
  279.2 10.6 %copy-start.20 = (s32[32]{0:T(128)S(1)}, s32[32]{0:T(128)}, u32[]{:S(2)}) copy-start(s32[32]{0:T(128)} %param.27) | copy-start | bytes 388
  279.2 10.6 %copy-start.14 = (s32[32]{0:T(128)S(1)}, s32[32]{0:T(128)}, u32[]{:S(2)}) copy-start(s32[32]{0:T(128)} %copy-done.13) | copy-start | bytes 388
  284.9 11.9 %all-to-all-start.2 = ((bf16[32,4,640]{2,1,0:T(4,128)(2,1)}), bf16[32,4,640]{2,1,0:T(4,128)(2,1)S(1)}, u32[]{:S(2)}, u32[]{:S(2)}) async-start(bf16[32,4,640]{2,1,0:T(4,128)(2,1)} %convert_element_type.90), calls=%async_computation.3 | async-start | bytes 327680 | tf_op jit(solution)/shard_map/all_to_all | solution.py:243
  289.8 62.2 %all-gather.6.cloned.1.call-start = ((), (), s32[]{:S(2)}) async-start(), calls=%async_computation.9 | async-start | bytes 3538944 | tf_op jit(solution)/shard_map/all_gather | solution.py:337
  311.2 79.1 %reduce-scatter.12.cloned.1.call-start = ((), (), s32[]{:S(2)}) async-start(), calls=%async_computation.11 | async-start | bytes 368640
  312.1 167.3 %reduce-scatter.10.cloned.1.call-start = ((), (), s32[]{:S(2)}) async-start(), calls=%async_computation.10 | async-start | bytes 2433024
  (8 other events, 20.7 us)
Sparse Core Ops, SparseCore 0:
  12.7 47.9 all-gather.3
  70.6 73.7 reduce-scatter.7
  311.3 40.6 all-gather.5
  354.4 35.8 reduce-scatter.11
  394.0 85.4 reduce-scatter.9
Sparse Core Ops, SparseCore 1:
  74.8 107.5 all-reduce.5

commit v3 on v2

--- a/solution.py
+++ b/solution.py
@@ -318,7 +318,13 @@
     active = frame_ids < frames_used
     mats = frame_matrices(blank_score, label_score, active)
     forward, backward_t = both_products(mats)
-    transfers = lax.all_gather(forward[-1], "section", axis=0, tiled=False)
+    transfers = lax.all_to_all(
+        jnp.broadcast_to(forward[-1][None], (section_count,) + forward.shape[1:]),
+        "section",
+        0,
+        0,
+        tiled=True,
+    )
     place_iota = jnp.arange(places, dtype=jnp.int32)
     start_vec = jnp.where(place_iota == 0, 0.0, NEG_BIG)
     finish_vec = jnp.where(place_iota == labels_used, 0.0, NEG_BIG)
@@ -355,7 +361,8 @@
     hidden_here = up_part.shape[1]
     up_sum = weight_sums[:, :hidden_here]
     down_sum = weight_sums[:, hidden_here:].T
-    pred_sum = lax.psum_scatter(pred_part[None], "section", scatter_dimension=2, tiled=True)
+    pred_pieces = jnp.swapaxes(pred_part.reshape(places, section_count, -1), 0, 1)
+    pred_sum = jnp.sum(lax.all_to_all(pred_pieces, "section", 0, 0, tiled=True), axis=0)[None]
     return (row_grad[None], up_sum, down_sum, pred_sum)
 
 

time: 491 us -> 453 us (0.923)
  waiting for transfers between devices: 282 us -> 252 us
  blocking collectives: 35.9 us -> 23.4 us
  starting transfers between devices: 19.7 us -> 26.7 us
    unnamed x9 -> x7, waiting for transfers between devices: 123 us -> 86.1 us
    all_gather x1 -> x0, blocking collectives: 24.3 us -> none  [on_device(): transfers = lax.all_gather(forward[-1], 'section', axis=0, tiled=False)]
    all_to_all x0 -> x1, blocking collectives: none -> 11.9 us  [on_device(): lax.all_to_all(pred_pieces, 'section', 0, 0, tiled=True)]
    all_to_all x0 -> x1, waiting for transfers between devices: none -> 7.67 us  [on_device(): lax.all_to_all(jnp.broadcast_to(forward[-1][None], (section_count,) + for...]
    all_to_all x0 -> x1, starting transfers between devices: none -> 7.01 us  [on_device(): lax.all_to_all(jnp.broadcast_to(forward[-1][None], (section_count,) + for...]
    unnamed x58 -> x60, local copies, waits for them, and re-layouts: 11.8 us -> 9.47 us
  transfers between devices with their start and end apart: 9 -> 9, of which waited for: 8 -> 8; matrix products, arithmetic and copies ran while one was open for 10% -> 7% of each run, Pallas kernels for 0% -> 0%
where the time goes in v3:
time: 453 us; the launch traced here: 451 us
  waiting for transfers between devices  252 us (56%)
  local copies, waits for them, and re-layouts  52 us (11%)
  matrix products  44.4 us (10%)
  other arithmetic  34 us (8%)
  starting transfers between devices  26.7 us (6%)
  blocking collectives  23.4 us (5%)
  between operations  18.7 us (4%)
    unnamed x7, waiting for transfers between devices  86.1 us
    reduce_scatter x1, waiting for transfers between devices, on_device(): lax.psum_scatter(0.5 * jnp.dot(hidden, down_weight, preferred_element_typ...  59.2 us
    all_gather x1, waiting for transfers between devices, on_device(): gathered = lax.all_gather(normed_in, 'section', axis=0, tiled=True)  48 us
    all_gather x1, waiting for transfers between devices, on_device(): grad_all = lax.all_gather(row_grad, 'section', axis=0, tiled=True)  38.5 us
    all_to_all x2, starting transfers between devices, route_rows(): spread = lax.all_to_all(payload, axis, 0, 0, tiled=True)  12.4 us
    dot_general x1, matrix products, joint_backward(): lax.dot_general(logit_grad, output_proj, (((1,), (1,)), ((), ())), prefer...  12.4 us
    all_to_all x1, blocking collectives, on_device(): lax.all_to_all(pred_pieces, 'section', 0, 0, tiled=True)  11.9 us
    all_to_all x1, blocking collectives, route_rows(): return lax.all_to_all(picked, axis, 0, 0, tiled=True)  11.5 us
  transfers between devices with their start and end apart: 9, of which 8 were waited for; matrix products, arithmetic and copies ran while one was open for 7% of the time, Pallas kernels for 0%

profile of v3, /device:TPU:2, one launch (start us, length us, event | category | flops | bytes accessed | tf_op | source)
XLA Modules:
  0.0 451.2 jit_solution(3486738073775288264)
XLA Ops:
  12.7 48.0 %all-gather.3.cloned.1.call-done = bf16[1024,1536]{1,0:T(8,128)(2,1)} async-done(((bf16[128,1536]{1,0:T(8,128)(2,1)}), bf16[1024,1536]{1,0:T(8,128)(2,1)}) %all-gather.3.cloned.1.call-update) | async-done | bytes 3145744 | tf_op jit(solution)/shard_map/all_gather | solution.py:273
  60.7 3.8 fusion.83
  65.7 4.5 convolution_multiply_fusion
  85.0 59.2 %reduce-scatter.5.cloned.1.call-done = f32[128,1536]{1,0:T(8,128)} async-done(((f32[1024,1536]{1,0:T(8,128)}), f32[128,1536]{1,0:T(8,128)}) %reduce-scatter.5.cloned.1.call-update) | async-done | bytes 786448 | tf_op jit(solution)/shard_map/reduce_scatter | solution.py:276
  148.2 7.4 %all-to-all-start = ((bf16[32,4,640]{2,1,0:T(4,128)(2,1)}), bf16[32,4,640]{2,1,0:T(4,128)(2,1)S(1)}, u32[]{:S(2)}, u32[]{:S(2)}) async-start(bf16[32,4,640]{2,1,0:T(4,128)(2,1)} %all_to_all.26), calls=%async_computation.1 | async-start | bytes 327680 | tf_op jit(solution)/shard_map/all_to_all | solution.py:243
  160.9 6.8 %broadcast_in_dim.329 = pred[512,4096]{1,0:T(32,128)(4,1)} reshape(pred[128,4,4096]{2,1,0:T(4,128)(4,1)} %broadcast_in_dim.328) | data formatting | bytes 4194304 | tf_op jit(solution)/shard_map/jit(_where)/broadcast_in_dim | solution.py:184
  168.9 13.2 %all-reduce.6.cloned.1.call-done = bf16[128,640]{1,0:T(8,128)(2,1)} async-done(((bf16[128,640]{1,0:T(8,128)(2,1)}), bf16[128,640]{1,0:T(8,128)(2,1)}) %all-reduce.6.cloned.1.call-update) | async-done | bytes 163856
  184.4 6.9 %all-to-all-start.1 = ((bf16[32,4,640]{2,1,0:T(4,128)(2,1)}), bf16[32,4,640]{2,1,0:T(4,128)(2,1)}, u32[]{:S(2)}, u32[]{:S(2)}) async-start(bf16[32,4,640]{2,1,0:T(4,128)(2,1)} %broadcast_select_fusion.1), calls=%async_computation.2 | async-start | bytes 327680 | tf_op jit(solution)/shard_map/all_to_all | solution.py:246
  192.7 5.5 %all-to-all-done.1 = bf16[32,4,640]{2,1,0:T(4,128)(2,1)} async-done(((bf16[32,4,640]{2,1,0:T(4,128)(2,1)}), bf16[32,4,640]{2,1,0:T(4,128)(2,1)}, u32[]{:S(2)}, u32[]{:S(2)}) %all-to-all-start.1) | async-done | bytes 163872 | tf_op jit(solution)/shard_map/all_to_all | solution.py:246
  202.5 9.4 %exponential_reduce_fusion = (f32[512]{0:T(512)S(1)}, f32[512,4096]{1,0:T(8,128)}) fusion(f32[4096]{0:T(1024)} %param.23, bf16[512,640]{1,0:T(8,128)(2,1)} %convert_element_type.86, bf16[640,4096]{1,0:T(8,128)(2,1)} %param.22), kind=kOutput, calls=%fused_computation.6 | convolution fusion | flops 2688548352 | bytes 14305280 | tf_op jit(solution)/shard_map/dot_general | solution.py:158
  211.9 9.8 %reshape.821 = f32[128,4,4096]{2,1,0:T(4,128)} reshape(f32[512,4096]{1,0:T(8,128)} %get-tuple-element.42) | data formatting | bytes 16777216 | tf_op jit(solution)/shard_map/reshape | solution.py:165
  222.7 5.5 %gather_fusion.1 = f32[384]{0:T(512)S(1)} fusion(f32[128,3,4096]{2,1,0:T(4,128)} %bitcast.111, s32[384]{0:T(512)S(1)} %reshape.851), kind=kCustom, calls=%fused_computation.3 | custom fusion | bytes 7680 | tf_op jit(solution)/shard_map/jit(take_along_axis)/gather | solution.py:171
  236.5 7.0 %all-to-all-start.2 = ((f32[8,4,4]{1,2,0:T(4,128)}), f32[8,4,4]{1,2,0:T(4,128)S(1)}, u32[]{:S(2)}, u32[]{:S(2)}) async-start(f32[8,4,4]{1,2,0:T(4,128)} %broadcast_in_dim.320), calls=%async_computation.3 | async-start | bytes 32768 | tf_op jit(solution)/shard_map/all_to_all | solution.py:321
  243.6 7.7 %all-to-all-done.2 = f32[8,4,4]{1,2,0:T(4,128)S(1)} async-done(((f32[8,4,4]{1,2,0:T(4,128)}), f32[8,4,4]{1,2,0:T(4,128)S(1)}, u32[]{:S(2)}, u32[]{:S(2)}) %all-to-all-start.2) | async-done | bytes 544 | tf_op jit(solution)/shard_map/all_to_all | solution.py:321
  256.5 12.4 %fusion.2 = f32[512,640]{1,0:T(8,128)} fusion(bf16[640,4096]{1,0:T(8,128)(2,1)} %param.22, pred[512,4096]{1,0:T(32,128)(4,1)} %broadcast_in_dim.329, f32[512,4096]{1,0:T(8,128)} %get-tuple-element.42, f32[512]{0:T(512)S(1)} %broadcast_in_dim.330, f32[512]{0:T(512)S(1)} %neg.26, f32[512]{0:T(512)S(1)} %mul.131, f32[512]{0:T(512)S(1)} %get-tuple-element.41, ...), kind=kOutput, calls=%fused_computation.17 | convolution fusion | flops 2702442496 | bytes 17707008 | tf_op jit(solution)/shard_map/dot_general | solution.py:187
  274.4 5.0 %all-to-all-start.3 = ((bf16[32,4,640]{2,1,0:T(4,128)(2,1)}), bf16[32,4,640]{2,1,0:T(4,128)(2,1)S(1)}, u32[]{:S(2)}, u32[]{:S(2)}) async-start(bf16[32,4,640]{2,1,0:T(4,128)(2,1)} %convert_element_type.90), calls=%async_computation.4 | async-start | bytes 327680 | tf_op jit(solution)/shard_map/all_to_all | solution.py:243
  279.5 6.8 %all-to-all-done.3 = bf16[32,4,640]{2,1,0:T(4,128)(2,1)S(1)} async-done(((bf16[32,4,640]{2,1,0:T(4,128)(2,1)}), bf16[32,4,640]{2,1,0:T(4,128)(2,1)S(1)}, u32[]{:S(2)}, u32[]{:S(2)}) %all-to-all-start.3) | async-done | bytes 163872 | tf_op jit(solution)/shard_map/all_to_all | solution.py:243
  287.2 11.5 %all_to_all.40 = bf16[32,4,640]{2,1,0:T(4,128)(2,1)S(1)} all-to-all(bf16[32,4,640]{2,1,0:T(4,128)(2,1)S(1)} %broadcast_select_fusion), channel_id=1, replica_groups=mesh['section'=8,'joint'=32] {'joint'}, dimensions={0} | all-to-all | bytes 327680 | tf_op jit(solution)/shard_map/all_to_all | solution.py:246
  301.1 38.5 %all-gather.5.cloned.1.call-done = bf16[1024,1536]{1,0:T(8,128)(2,1)} async-done(((bf16[128,1536]{1,0:T(8,128)(2,1)}), bf16[1024,1536]{1,0:T(8,128)(2,1)}) %all-gather.5.cloned.1.call-update) | async-done | bytes 3145744 | tf_op jit(solution)/shard_map/all_gather | solution.py:343
  339.6 6.8 %convolution_convert_fusion = bf16[1536,384]{0,1:T(8,128)(2,1)S(1)} fusion(bf16[1024,1536]{1,0:T(8,128)(2,1)} %all-gather.3.cloned.1.call-done, f32[1024,384]{1,0:T(8,128)} %copy-done.24, bf16[1024,1536]{1,0:T(8,128)(2,1)} %all-gather.5.cloned.1.call-done, bf16[384,1536]{1,0:T(8,128)(2,1)} %param.17), kind=kOutput, calls=%fused_computation.12 | convolution fusion | flops 2420441088 | bytes 10223616 | tf_op jit(solution)/shard_map/dot_general | solution.py:351
  346.4 3.8 fusion.1
  351.8 4.3 copy.185
  356.2 11.9 %all_to_all.41 = f32[8,4,80]{2,1,0:T(4,128)S(1)} all-to-all(f32[8,4,80]{2,1,0:T(4,128)S(1)} %copy.181), channel_id=1, replica_groups=mesh['section'=8,'joint'=32] {'section'}, dimensions={0} | all-to-all | bytes 20480 | tf_op jit(solution)/shard_map/all_to_all | solution.py:365
  368.7 72.8 %reduce-scatter.7.cloned.1.call-done = bf16[48,768]{1,0:T(8,128)(2,1)} async-done(((bf16[1536,768]{1,0:T(8,128)(2,1)}), bf16[48,768]{1,0:T(8,128)(2,1)}) %reduce-scatter.7.cloned.1.call-update) | async-done | bytes 73744
  (266 shorter events, 64.1 us)
Async XLA Ops:
  8.0 138.9 %copy-start = (bf16[1536,640]{1,0:T(8,128)(2,1)S(1)}, bf16[1536,640]{1,0:T(8,128)(2,1)}, u32[]{:S(2)}) copy-start(bf16[1536,640]{1,0:T(8,128)(2,1)} %param.18) | copy-start | bytes 5898244
  8.0 52.7 %copy-start.17 = (bf16[1536,384]{1,0:T(8,128)(2,1)S(1)}, bf16[1536,384]{1,0:T(8,128)(2,1)}, u32[]{:S(2)}) copy-start(bf16[1536,384]{1,0:T(8,128)(2,1)} %param.16) | copy-start | bytes 3538948
  8.0 52.7 %all-gather.3.cloned.1.call-start = ((), (), s32[]{:S(2)}) async-start(), calls=%async_computation.8 | async-start | bytes 3538944 | tf_op jit(solution)/shard_map/all_gather | solution.py:273
  12.6 131.5 %reduce-scatter.5.cloned.1.call-start = ((), (), s32[]{:S(2)}) async-start(), calls=%async_computation.9 | async-start | bytes 7077888 | tf_op jit(solution)/shard_map/reduce_scatter | solution.py:276
  70.2 12.2 %copy-start.5 = (f32[2,640]{1,0:T(2,128)S(1)}, f32[2,640]{1,0:T(2,128)}, u32[]{:S(2)}) copy-start(f32[2,640]{1,0:T(2,128)} %param.20) | copy-start | bytes 15364
  70.2 12.3 %copy-start.19 = (s32[32]{0:T(128)S(1)}, s32[32]{0:T(128)}, u32[]{:S(2)}) copy-start(s32[32]{0:T(128)} %param.24) | copy-start | bytes 388
  70.2 12.9 %copy-start.20 = (s32[32]{0:T(128)S(1)}, s32[32]{0:T(128)}, u32[]{:S(2)}) copy-start(s32[32]{0:T(128)} %param.25) | copy-start | bytes 388
  70.2 73.9 %copy-start.1 = (bf16[1,128,1536]{2,1,0:T(8,128)(2,1)S(1)}, bf16[1,128,1536]{2,1,0:T(8,128)(2,1)}, u32[]{:S(2)}) copy-start(bf16[1,128,1536]{2,1,0:T(8,128)(2,1)} %param.15) | copy-start | bytes 1179652
  70.3 111.9 %all-reduce.6.cloned.1.call-start = ((), (), s32[]{:S(2)}) async-start(), calls=%async_computation.12 | async-start | bytes 327680
  76.2 6.3 %copy-start.9 = (s32[3]{0:T(128)}, s32[3]{0:T(128)S(1)}, u32[]{:S(2)}) copy-start(s32[3]{0:T(128)S(1)} %broadcast_add_fusion) | copy-start | bytes 40
  76.2 69.4 %copy-start.11 = (pred[3]{0:T(512)(128)(4,1)}, pred[3]{0:T(512)(128)(4,1)S(1)}, u32[]{:S(2)}) copy-start(pred[3]{0:T(512)(128)(4,1)S(1)} %broadcast_compare_fusion) | copy-start | bytes 13
  148.2 34.7 %all-to-all-start = ((bf16[32,4,640]{2,1,0:T(4,128)(2,1)}), bf16[32,4,640]{2,1,0:T(4,128)(2,1)S(1)}, u32[]{:S(2)}, u32[]{:S(2)}) async-start(bf16[32,4,640]{2,1,0:T(4,128)(2,1)} %all_to_all.26), calls=%async_computation.1 | async-start | bytes 327680 | tf_op jit(solution)/shard_map/all_to_all | solution.py:243
  160.9 6.8 %copy-start.23 = (u32[256]{0:T(256)S(1)}, u32[256]{0:T(256)}, u32[]{:S(2)}) copy-start(u32[256]{0:T(256)} %constant.132) | copy-start | bytes 3076
  160.9 22.7 %copy-start.14 = (pred[32]{0:T(512)(128)(4,1)S(1)}, pred[32]{0:T(512)(128)(4,1)}, u32[]{:S(2)}) copy-start(pred[32]{0:T(512)(128)(4,1)} %compare_and_fusion.1) | copy-start | bytes 100
  184.4 13.8 %all-to-all-start.1 = ((bf16[32,4,640]{2,1,0:T(4,128)(2,1)}), bf16[32,4,640]{2,1,0:T(4,128)(2,1)}, u32[]{:S(2)}, u32[]{:S(2)}) async-start(bf16[32,4,640]{2,1,0:T(4,128)(2,1)} %broadcast_select_fusion.1), calls=%async_computation.2 | async-start | bytes 327680 | tf_op jit(solution)/shard_map/all_to_all | solution.py:246
  228.2 25.2 %copy-start.13 = (pred[8]{0:T(512)(128)(4,1)S(1)}, pred[8]{0:T(512)(128)(4,1)}, u32[]{:S(2)}) copy-start(pred[8]{0:T(512)(128)(4,1)} %iota_compare_fusion.17) | copy-start | bytes 28
  228.2 25.9 %copy-start.8 = (f32[4]{0:T(128)S(1)}, f32[4]{0:T(128)}, u32[]{:S(2)}) copy-start(f32[4]{0:T(128)} %compare_select_fusion.2) | copy-start | bytes 52
  236.5 14.8 %all-to-all-start.2 = ((f32[8,4,4]{1,2,0:T(4,128)}), f32[8,4,4]{1,2,0:T(4,128)S(1)}, u32[]{:S(2)}, u32[]{:S(2)}) async-start(f32[8,4,4]{1,2,0:T(4,128)} %broadcast_in_dim.320), calls=%async_computation.3 | async-start | bytes 32768 | tf_op jit(solution)/shard_map/all_to_all | solution.py:321
  268.8 10.6 %copy-start.22 = (s32[32]{0:T(128)S(1)}, s32[32]{0:T(128)}, u32[]{:S(2)}) copy-start(s32[32]{0:T(128)} %param.27) | copy-start | bytes 388
  268.8 10.6 %copy-start.16 = (s32[32]{0:T(128)S(1)}, s32[32]{0:T(128)}, u32[]{:S(2)}) copy-start(s32[32]{0:T(128)} %copy-done.15) | copy-start | bytes 388
  271.5 27.3 %copy-start.7 = (f32[128]{0:T(128)S(1)}, f32[128]{0:T(128)}, u32[]{:S(2)}) copy-start(f32[128]{0:T(128)} %copy-done.6) | copy-start | bytes 1540
  274.4 11.9 %all-to-all-start.3 = ((bf16[32,4,640]{2,1,0:T(4,128)(2,1)}), bf16[32,4,640]{2,1,0:T(4,128)(2,1)S(1)}, u32[]{:S(2)}, u32[]{:S(2)}) async-start(bf16[32,4,640]{2,1,0:T(4,128)(2,1)} %convert_element_type.90), calls=%async_computation.4 | async-start | bytes 327680 | tf_op jit(solution)/shard_map/all_to_all | solution.py:243
  279.4 60.2 %all-gather.5.cloned.1.call-start = ((), (), s32[]{:S(2)}) async-start(), calls=%async_computation.10 | async-start | bytes 3538944 | tf_op jit(solution)/shard_map/all_gather | solution.py:343
  300.8 140.7 %reduce-scatter.7.cloned.1.call-start = ((), (), s32[]{:S(2)}) async-start(), calls=%async_computation.11 | async-start | bytes 2433024
  (10 other events, 26.9 us)
Sparse Core Ops, SparseCore 0:
  12.8 47.9 all-gather.2
  70.4 73.7 reduce-scatter.4
  300.9 38.6 all-gather.4
Sparse Core Ops, SparseCore 1:
  74.6 107.5 all-reduce.5
  356.1 85.3 reduce-scatter.6

commit v4 on v3

--- a/solution.py
+++ b/solution.py
@@ -355,8 +355,9 @@
         hidden, grad_all, (((0,), (0,)), ((), ())), preferred_element_type=jnp.float32
     )
     weight_parts = jnp.concatenate([up_part, down_part.T], axis=1).astype(jnp.bfloat16)
-    weight_sums = lax.psum_scatter(weight_parts, "joint", scatter_dimension=0, tiled=True).astype(
-        jnp.float32
+    weight_pieces = lax.all_to_all(weight_parts, "joint", 0, 0, tiled=True)
+    weight_sums = jnp.sum(
+        weight_pieces.reshape(joint_count, -1, weight_parts.shape[1]).astype(jnp.float32), axis=0
     )
     hidden_here = up_part.shape[1]
     up_sum = weight_sums[:, :hidden_here]

time: 453 us -> 405 us (0.89)
  waiting for transfers between devices: 252 us -> 205 us
  blocking collectives: 23.4 us -> 11.5 us
  starting transfers between devices: 26.7 us -> 37.2 us
  local copies, waits for them, and re-layouts: 52 us -> 46.5 us
    unnamed x7 -> x5, waiting for transfers between devices: 86.1 us -> 13.3 us
    all_to_all x0 -> x2, waiting for transfers between devices: none -> 30.3 us  [the longest x1 30.3 us: on_device(): weight_pieces = lax.all_to_all(weight_parts, 'joint', 0, 0, tiled=True)]
    all_to_all x1 -> x0, blocking collectives: 11.9 us -> none  [on_device(): lax.all_to_all(pred_pieces, 'section', 0, 0, tiled=True)]
    all_to_all x0 -> x2, starting transfers between devices: none -> 10.9 us  [the longest x1 7.26 us: on_device(): weight_pieces = lax.all_to_all(weight_parts, 'joint', 0, 0, tiled=True)]
    unnamed x60 -> x56, local copies, waits for them, and re-layouts: 9.47 us -> 2.67 us
  transfers between devices with their start and end apart: 9 -> 10, of which waited for: 8 -> 8; matrix products, arithmetic and copies ran while one was open for 7% -> 11% of each run, Pallas kernels for 0% -> 0%
where the time goes in v4:
time: 405 us; the launch traced here: 402 us
  waiting for transfers between devices  205 us (51%)
  local copies, waits for them, and re-layouts  46.5 us (11%)
  matrix products  45.4 us (11%)
  other arithmetic  37.8 us (9%)
  starting transfers between devices  37.2 us (9%)
  between operations  18.7 us (5%)
  blocking collectives  11.5 us (3%)
    reduce_scatter x1, waiting for transfers between devices, on_device(): lax.psum_scatter(0.5 * jnp.dot(hidden, down_weight, preferred_element_typ...  58.7 us
    all_gather x1, waiting for transfers between devices, on_device(): gathered = lax.all_gather(normed_in, 'section', axis=0, tiled=True)  48 us
    all_gather x1, waiting for transfers between devices, on_device(): grad_all = lax.all_gather(row_grad, 'section', axis=0, tiled=True)  34.8 us
    all_to_all x1, waiting for transfers between devices, on_device(): weight_pieces = lax.all_to_all(weight_parts, 'joint', 0, 0, tiled=True)  30.3 us
    unnamed x5, waiting for transfers between devices  13.3 us
    all_to_all x2, starting transfers between devices, route_rows(): spread = lax.all_to_all(payload, axis, 0, 0, tiled=True)  12.3 us
    dot_general x1, matrix products, joint_backward(): lax.dot_general(logit_grad, output_proj, (((1,), (1,)), ((), ())), prefer...  12.3 us
    all_to_all x1, blocking collectives, route_rows(): return lax.all_to_all(picked, axis, 0, 0, tiled=True)  11.5 us
  transfers between devices with their start and end apart: 10, of which 8 were waited for; matrix products, arithmetic and copies ran while one was open for 11% of the time, Pallas kernels for 0%

profile of v4, /device:TPU:2, one launch (start us, length us, event | category | flops | bytes accessed | tf_op | source)
XLA Modules:
  0.0 402.2 jit_solution(16881020995816559820)
XLA Ops:
  12.7 48.0 %all-gather.3.cloned.1.call-done = bf16[1024,1536]{1,0:T(8,128)(2,1)} async-done(((bf16[128,1536]{1,0:T(8,128)(2,1)}), bf16[1024,1536]{1,0:T(8,128)(2,1)}) %all-gather.3.cloned.1.call-update) | async-done | bytes 3145744 | tf_op jit(solution)/shard_map/all_gather | solution.py:273
  60.7 4.0 fusion.83
  65.9 4.5 %convolution_multiply_fusion = f32[1024,1536]{1,0:T(8,128)} fusion(bf16[384,1536]{1,0:T(8,128)(2,1)S(1)} %copy-done.18, f32[1024,384]{1,0:T(8,128)S(1)} %fusion.83), kind=kOutput, calls=%fused_computation.9 | convolution fusion | flops 1211498496 | bytes 9043968 | tf_op jit(solution)/shard_map/dot_general | solution.py:277
  85.7 58.7 %reduce-scatter.2.cloned.1.call-done = f32[128,1536]{1,0:T(8,128)} async-done(((f32[1024,1536]{1,0:T(8,128)}), f32[128,1536]{1,0:T(8,128)}) %reduce-scatter.2.cloned.1.call-update) | async-done | bytes 786448 | tf_op jit(solution)/shard_map/reduce_scatter | solution.py:276
  148.4 7.4 %all-to-all-start = ((bf16[32,4,640]{2,1,0:T(4,128)(2,1)}), bf16[32,4,640]{2,1,0:T(4,128)(2,1)S(1)}, u32[]{:S(2)}, u32[]{:S(2)}) async-start(bf16[32,4,640]{2,1,0:T(4,128)(2,1)} %all_to_all.30), calls=%async_computation.1 | async-start | bytes 327680 | tf_op jit(solution)/shard_map/all_to_all | solution.py:243
  161.0 6.8 %broadcast_in_dim.329 = pred[512,4096]{1,0:T(32,128)(4,1)} reshape(pred[128,4,4096]{2,1,0:T(4,128)(4,1)} %broadcast_in_dim.328) | data formatting | bytes 4194304 | tf_op jit(solution)/shard_map/jit(_where)/broadcast_in_dim | solution.py:184
  169.1 13.2 %all-reduce.6.cloned.1.call-done = bf16[128,640]{1,0:T(8,128)(2,1)} async-done(((bf16[128,640]{1,0:T(8,128)(2,1)}), bf16[128,640]{1,0:T(8,128)(2,1)}) %all-reduce.6.cloned.1.call-update) | async-done | bytes 163856
  184.6 6.9 %all-to-all-start.1 = ((bf16[32,4,640]{2,1,0:T(4,128)(2,1)}), bf16[32,4,640]{2,1,0:T(4,128)(2,1)}, u32[]{:S(2)}, u32[]{:S(2)}) async-start(bf16[32,4,640]{2,1,0:T(4,128)(2,1)} %broadcast_select_fusion.1), calls=%async_computation.2 | async-start | bytes 327680 | tf_op jit(solution)/shard_map/all_to_all | solution.py:246
  192.9 5.5 %all-to-all-done.1 = bf16[32,4,640]{2,1,0:T(4,128)(2,1)} async-done(((bf16[32,4,640]{2,1,0:T(4,128)(2,1)}), bf16[32,4,640]{2,1,0:T(4,128)(2,1)}, u32[]{:S(2)}, u32[]{:S(2)}) %all-to-all-start.1) | async-done | bytes 163872 | tf_op jit(solution)/shard_map/all_to_all | solution.py:246
  202.7 9.4 %exponential_reduce_fusion = (f32[512]{0:T(512)S(1)}, f32[512,4096]{1,0:T(8,128)}) fusion(f32[4096]{0:T(1024)} %param.23, bf16[512,640]{1,0:T(8,128)(2,1)} %convert_element_type.87, bf16[640,4096]{1,0:T(8,128)(2,1)} %param.22), kind=kOutput, calls=%fused_computation.6 | convolution fusion | flops 2688548352 | bytes 14305280 | tf_op jit(solution)/shard_map/dot_general | solution.py:158
  212.1 9.8 %reshape.829 = f32[128,4,4096]{2,1,0:T(4,128)} reshape(f32[512,4096]{1,0:T(8,128)} %get-tuple-element.24) | data formatting | bytes 16777216 | tf_op jit(solution)/shard_map/reshape | solution.py:165
  222.9 5.5 %gather_fusion.1 = f32[384]{0:T(512)S(1)} fusion(f32[128,3,4096]{2,1,0:T(4,128)} %bitcast.112, s32[384]{0:T(512)S(1)} %reshape.859), kind=kCustom, calls=%fused_computation.3 | custom fusion | bytes 7680 | tf_op jit(solution)/shard_map/jit(take_along_axis)/gather | solution.py:171
  236.7 7.0 %all-to-all-start.2 = ((f32[8,4,4]{1,2,0:T(4,128)}), f32[8,4,4]{1,2,0:T(4,128)S(1)}, u32[]{:S(2)}, u32[]{:S(2)}) async-start(f32[8,4,4]{1,2,0:T(4,128)} %broadcast_in_dim.320), calls=%async_computation.3 | async-start | bytes 32768 | tf_op jit(solution)/shard_map/all_to_all | solution.py:321
  243.8 7.7 %all-to-all-done.2 = f32[8,4,4]{1,2,0:T(4,128)S(1)} async-done(((f32[8,4,4]{1,2,0:T(4,128)}), f32[8,4,4]{1,2,0:T(4,128)S(1)}, u32[]{:S(2)}, u32[]{:S(2)}) %all-to-all-start.2) | async-done | bytes 544 | tf_op jit(solution)/shard_map/all_to_all | solution.py:321
  258.0 12.3 %fusion.2 = f32[512,640]{1,0:T(8,128)} fusion(bf16[640,4096]{1,0:T(8,128)(2,1)} %param.22, pred[512,4096]{1,0:T(32,128)(4,1)} %broadcast_in_dim.329, f32[512,4096]{1,0:T(8,128)} %get-tuple-element.24, f32[512]{0:T(512)S(1)} %broadcast_in_dim.330, f32[512]{0:T(512)S(1)} %neg.26, f32[512]{0:T(512)S(1)} %mul.131, f32[512]{0:T(512)S(1)} %copy-done.7, ...), kind=kOutput, calls=%fused_computation.18 | convolution fusion | flops 2702442496 | bytes 17707008 | tf_op jit(solution)/shard_map/dot_general | solution.py:187
  275.9 4.9 %all-to-all-start.3 = ((bf16[32,4,640]{2,1,0:T(4,128)(2,1)}), bf16[32,4,640]{2,1,0:T(4,128)(2,1)S(1)}, u32[]{:S(2)}, u32[]{:S(2)}) async-start(bf16[32,4,640]{2,1,0:T(4,128)(2,1)} %convert_element_type.91), calls=%async_computation.4 | async-start | bytes 327680 | tf_op jit(solution)/shard_map/all_to_all | solution.py:243
  280.9 6.8 %all-to-all-done.3 = bf16[32,4,640]{2,1,0:T(4,128)(2,1)S(1)} async-done(((bf16[32,4,640]{2,1,0:T(4,128)(2,1)}), bf16[32,4,640]{2,1,0:T(4,128)(2,1)S(1)}, u32[]{:S(2)}, u32[]{:S(2)}) %all-to-all-start.3) | async-done | bytes 163872 | tf_op jit(solution)/shard_map/all_to_all | solution.py:243
  288.6 11.5 %all_to_all.46 = bf16[32,4,640]{2,1,0:T(4,128)(2,1)S(1)} all-to-all(bf16[32,4,640]{2,1,0:T(4,128)(2,1)S(1)} %broadcast_select_fusion), channel_id=1, replica_groups=mesh['section'=8,'joint'=32] {'joint'}, dimensions={0} | all-to-all | bytes 327680 | tf_op jit(solution)/shard_map/all_to_all | solution.py:246
  302.9 3.6 all-to-all-start.6
  306.5 34.8 %all-gather.5.cloned.1.call-done = bf16[1024,1536]{1,0:T(8,128)(2,1)} async-done(((bf16[128,1536]{1,0:T(8,128)(2,1)}), bf16[1024,1536]{1,0:T(8,128)(2,1)}) %all-gather.5.cloned.1.call-update) | async-done | bytes 3145744 | tf_op jit(solution)/shard_map/all_gather | solution.py:343
  341.2 7.1 %convolution_convert_fusion = bf16[1536,384]{1,0:T(8,128)(2,1)S(1)} fusion(bf16[1024,1536]{1,0:T(8,128)(2,1)} %all-gather.3.cloned.1.call-done, f32[1024,384]{1,0:T(8,128)} %copy-done.24, bf16[1024,1536]{1,0:T(8,128)(2,1)} %all-gather.5.cloned.1.call-done, bf16[384,1536]{1,0:T(8,128)(2,1)} %param.17), kind=kOutput, calls=%fused_computation.13 | convolution fusion | flops 2420441088 | bytes 10223616 | tf_op jit(solution)/shard_map/dot_general | solution.py:351
  348.4 4.2 %fusion.1 = bf16[1536,384]{1,0:T(8,128)(2,1)S(1)} fusion(bf16[1024,1536]{1,0:T(8,128)(2,1)} %all-gather.5.cloned.1.call-done, f32[1024,384]{1,0:T(8,128)} %copy-done.24), kind=kOutput, calls=%fused_computation.12 | convolution fusion | flops 1211105280 | bytes 5898240 | tf_op jit(solution)/shard_map/dot_general | solution.py:354
  354.2 7.3 %all-to-all-start.5 = ((bf16[32,48,768]{2,1,0:T(8,128)(2,1)}), bf16[32,48,768]{2,1,0:T(8,128)(2,1)}, u32[]{:S(2)}, u32[]{:S(2)}) async-start(bf16[32,48,768]{2,1,0:T(8,128)(2,1)} %pad_maximum_fusion), calls=%async_computation.6 | async-start | bytes 4718592 | tf_op jit(solution)/shard_map/all_to_all | solution.py:358
  362.1 30.3 %all-to-all-done.5 = bf16[32,48,768]{2,1,0:T(8,128)(2,1)} async-done(((bf16[32,48,768]{2,1,0:T(8,128)(2,1)}), bf16[32,48,768]{2,1,0:T(8,128)(2,1)}, u32[]{:S(2)}, u32[]{:S(2)}) %all-to-all-start.5) | async-done | bytes 2359328 | tf_op jit(solution)/shard_map/all_to_all | solution.py:358
  (261 shorter events, 66.2 us)
Async XLA Ops:
  8.0 139.1 %copy-start = (bf16[1536,640]{1,0:T(8,128)(2,1)S(1)}, bf16[1536,640]{1,0:T(8,128)(2,1)}, u32[]{:S(2)}) copy-start(bf16[1536,640]{1,0:T(8,128)(2,1)} %param.18) | copy-start | bytes 5898244
  8.0 52.7 %all-gather.3.cloned.1.call-start = ((), (), s32[]{:S(2)}) async-start(), calls=%async_computation.8 | async-start | bytes 3538944 | tf_op jit(solution)/shard_map/all_gather | solution.py:273
  12.6 53.3 %copy-start.18 = (bf16[384,1536]{1,0:T(8,128)(2,1)S(1)}, bf16[384,1536]{1,0:T(8,128)(2,1)}, u32[]{:S(2)}) copy-start(bf16[384,1536]{1,0:T(8,128)(2,1)} %param.17) | copy-start | bytes 3538948
  12.6 131.8 %reduce-scatter.2.cloned.1.call-start = ((), (), s32[]{:S(2)}) async-start(), calls=%async_computation.9 | async-start | bytes 7077888 | tf_op jit(solution)/shard_map/reduce_scatter | solution.py:276
  70.4 12.8 %copy-start.5 = (f32[2,640]{1,0:T(2,128)S(1)}, f32[2,640]{1,0:T(2,128)}, u32[]{:S(2)}) copy-start(f32[2,640]{1,0:T(2,128)} %param.20) | copy-start | bytes 15364
  70.4 12.8 %copy-start.19 = (s32[32]{0:T(128)S(1)}, s32[32]{0:T(128)}, u32[]{:S(2)}) copy-start(s32[32]{0:T(128)} %param.24) | copy-start | bytes 388
  70.4 13.4 %copy-start.20 = (s32[32]{0:T(128)S(1)}, s32[32]{0:T(128)}, u32[]{:S(2)}) copy-start(s32[32]{0:T(128)} %param.25) | copy-start | bytes 388
  70.4 73.9 %copy-start.1 = (bf16[1,128,1536]{2,1,0:T(8,128)(2,1)S(1)}, bf16[1,128,1536]{2,1,0:T(8,128)(2,1)}, u32[]{:S(2)}) copy-start(bf16[1,128,1536]{2,1,0:T(8,128)(2,1)} %param.15) | copy-start | bytes 1179652
  70.5 111.9 %all-reduce.6.cloned.1.call-start = ((), (), s32[]{:S(2)}) async-start(), calls=%async_computation.11 | async-start | bytes 327680
  76.4 69.4 %copy-start.10 = (pred[3]{0:T(512)(128)(4,1)}, pred[3]{0:T(512)(128)(4,1)S(1)}, u32[]{:S(2)}) copy-start(pred[3]{0:T(512)(128)(4,1)S(1)} %broadcast_compare_fusion) | copy-start | bytes 13
  148.4 34.7 %all-to-all-start = ((bf16[32,4,640]{2,1,0:T(4,128)(2,1)}), bf16[32,4,640]{2,1,0:T(4,128)(2,1)S(1)}, u32[]{:S(2)}, u32[]{:S(2)}) async-start(bf16[32,4,640]{2,1,0:T(4,128)(2,1)} %all_to_all.30), calls=%async_computation.1 | async-start | bytes 327680 | tf_op jit(solution)/shard_map/all_to_all | solution.py:243
  161.0 22.7 %copy-start.15 = (pred[32]{0:T(512)(128)(4,1)S(1)}, pred[32]{0:T(512)(128)(4,1)}, u32[]{:S(2)}) copy-start(pred[32]{0:T(512)(128)(4,1)} %compare_and_fusion.1) | copy-start | bytes 100
  184.6 13.8 %all-to-all-start.1 = ((bf16[32,4,640]{2,1,0:T(4,128)(2,1)}), bf16[32,4,640]{2,1,0:T(4,128)(2,1)}, u32[]{:S(2)}, u32[]{:S(2)}) async-start(bf16[32,4,640]{2,1,0:T(4,128)(2,1)} %broadcast_select_fusion.1), calls=%async_computation.2 | async-start | bytes 327680 | tf_op jit(solution)/shard_map/all_to_all | solution.py:246
  212.1 16.6 %copy-start.6 = (f32[512]{0:T(512)}, f32[512]{0:T(512)S(1)}, u32[]{:S(2)}) copy-start(f32[512]{0:T(512)S(1)} %get-tuple-element.23) | copy-start | bytes 6148
  228.4 23.6 %copy-start.14 = (pred[8]{0:T(512)(128)(4,1)S(1)}, pred[8]{0:T(512)(128)(4,1)}, u32[]{:S(2)}) copy-start(pred[8]{0:T(512)(128)(4,1)} %iota_compare_fusion.15) | copy-start | bytes 28
  228.4 23.8 %copy-start.13 = (pred[8]{0:T(512)(128)(4,1)S(1)}, pred[8]{0:T(512)(128)(4,1)}, u32[]{:S(2)}) copy-start(pred[8]{0:T(512)(128)(4,1)} %iota_compare_fusion.16) | copy-start | bytes 28
  228.4 24.0 %copy-start.12 = (pred[8]{0:T(512)(128)(4,1)S(1)}, pred[8]{0:T(512)(128)(4,1)}, u32[]{:S(2)}) copy-start(pred[8]{0:T(512)(128)(4,1)} %iota_compare_fusion.17) | copy-start | bytes 28
  228.9 29.1 %copy-start.7 = (f32[512]{0:T(512)S(1)}, f32[512]{0:T(512)}, u32[]{:S(2)}) copy-start(f32[512]{0:T(512)} %copy-done.6) | copy-start | bytes 6148
  236.7 14.8 %all-to-all-start.2 = ((f32[8,4,4]{1,2,0:T(4,128)}), f32[8,4,4]{1,2,0:T(4,128)S(1)}, u32[]{:S(2)}, u32[]{:S(2)}) async-start(f32[8,4,4]{1,2,0:T(4,128)} %broadcast_in_dim.320), calls=%async_computation.3 | async-start | bytes 32768 | tf_op jit(solution)/shard_map/all_to_all | solution.py:321
  270.3 10.6 %copy-start.17 = (s32[32]{0:T(128)S(1)}, s32[32]{0:T(128)}, u32[]{:S(2)}) copy-start(s32[32]{0:T(128)} %copy-done.16) | copy-start | bytes 388
  275.9 11.9 %all-to-all-start.3 = ((bf16[32,4,640]{2,1,0:T(4,128)(2,1)}), bf16[32,4,640]{2,1,0:T(4,128)(2,1)S(1)}, u32[]{:S(2)}, u32[]{:S(2)}) async-start(bf16[32,4,640]{2,1,0:T(4,128)(2,1)} %convert_element_type.91), calls=%async_computation.4 | async-start | bytes 327680 | tf_op jit(solution)/shard_map/all_to_all | solution.py:243
  280.8 60.4 %all-gather.5.cloned.1.call-start = ((), (), s32[]{:S(2)}) async-start(), calls=%async_computation.10 | async-start | bytes 3538944 | tf_op jit(solution)/shard_map/all_gather | solution.py:343
  302.9 51.3 %all-to-all-start.6 = ((f32[8,4,80]{2,1,0:T(4,128)}), f32[8,4,80]{2,1,0:T(4,128)S(1)}, u32[]{:S(2)}, u32[]{:S(2)}) async-start(f32[8,4,80]{2,1,0:T(4,128)} %copy.173), calls=%async_computation.7 | async-start | bytes 32768 | tf_op jit(solution)/shard_map/all_to_all | solution.py:366
  354.2 38.2 %all-to-all-start.5 = ((bf16[32,48,768]{2,1,0:T(8,128)(2,1)}), bf16[32,48,768]{2,1,0:T(8,128)(2,1)}, u32[]{:S(2)}, u32[]{:S(2)}) async-start(bf16[32,48,768]{2,1,0:T(8,128)(2,1)} %pad_maximum_fusion), calls=%async_computation.6 | async-start | bytes 4718592 | tf_op jit(solution)/shard_map/all_to_all | solution.py:358
  (11 other events, 44.9 us)
Sparse Core Ops, SparseCore 0:
  12.7 47.9 all-gather.2
  70.6 73.7 reduce-scatter.1
  302.3 38.8 all-gather.4
Sparse Core Ops, SparseCore 1:
  74.8 107.5 all-reduce.5

commit v5 on v4

--- a/solution.py
+++ b/solution.py
@@ -273,12 +273,14 @@
     gathered = lax.all_gather(normed_in, "section", axis=0, tiled=True)
     pre_hidden = jnp.dot(gathered, up_weight, preferred_element_type=jnp.float32)
     hidden = jax.nn.silu(pre_hidden).astype(jnp.bfloat16)
-    encoded = own_rows + lax.psum_scatter(
+    output_pieces = lax.all_to_all(
         0.5 * jnp.dot(hidden, down_weight, preferred_element_type=jnp.float32),
         "section",
-        scatter_dimension=0,
+        0,
+        0,
         tiled=True,
     )
+    encoded = own_rows + jnp.sum(output_pieces.reshape(section_count, block_len, -1), axis=0)
     unit_rows, inv_scale = layer_norm(encoded)
     frame_part = jnp.dot(
         unit_rows.astype(jnp.bfloat16), encoder_proj, preferred_element_type=jnp.float32
@@ -297,12 +299,10 @@
         selector = (wanted[:, None] == vocab_ids[None, :]).astype(jnp.bfloat16)
         return jnp.dot(selector, embedding, preferred_element_type=jnp.float32)
 
-    looked = lax.psum_scatter(
-        label_term(jnp.int32(0), places * lax.axis_size("joint")).astype(jnp.bfloat16),
-        "joint",
-        scatter_dimension=0,
-        tiled=True,
-    ).astype(jnp.float32)
+    looked_pieces = lax.all_to_all(
+        label_term(jnp.int32(0), places * joint_count).astype(jnp.bfloat16), "joint", 0, 0, tiled=True
+    )
+    looked = jnp.sum(looked_pieces.reshape(joint_count, places, -1).astype(jnp.float32), axis=0)
     previous = jnp.concatenate([looked[:1], looked[:-1]], axis=0)
     pred_act = jnp.maximum(conv_taps[0] * previous + conv_taps[1] * looked, 0.0).astype(
         jnp.bfloat16

time: 405 us -> 465 us (1.15)
  waiting for transfers between devices: 205 us -> 261 us
  starting transfers between devices: 37.2 us -> 44.9 us
    all_to_all x0 -> x2, waiting for transfers between devices: none -> 128 us  [the longest x1 126 us: on_device(): lax.all_to_all(0.5 * jnp.dot(hidden, down_weight, preferred_element_type=...]
    reduce_scatter x1 -> x0, waiting for transfers between devices: 58.7 us -> none  [on_device(): lax.psum_scatter(0.5 * jnp.dot(hidden, down_weight, preferred_element_typ...]
    unnamed x5 -> x2, waiting for transfers between devices: 13.3 us -> 0.03 us
    all_to_all x0 -> x2, starting transfers between devices: none -> 12.3 us  [the longest x1 7.42 us: on_device(): lax.all_to_all(label_term(jnp.int32(0), places * joint_count).astype(jnp....]
  transfers between devices with their start and end apart: 10 -> 10, of which waited for: 8 -> 8; matrix products, arithmetic and copies ran while one was open for 11% -> 10% of each run, Pallas kernels for 0% -> 0%
where the time goes in v5:
time: 465 us; the launch traced here: 462 us
  waiting for transfers between devices  261 us (56%)
  local copies, waits for them, and re-layouts  46.1 us (10%)
  starting transfers between devices  44.9 us (10%)
  matrix products  44.7 us (10%)
  other arithmetic  37.5 us (8%)
  between operations  16.9 us (4%)
  blocking collectives  11.5 us (2%)
    all_to_all x1, waiting for transfers between devices, on_device(): lax.all_to_all(0.5 * jnp.dot(hidden, down_weight, preferred_element_type=...  126 us
    all_gather x1, waiting for transfers between devices, on_device(): gathered = lax.all_gather(normed_in, 'section', axis=0, tiled=True)  48.1 us
    all_gather x1, waiting for transfers between devices, on_device(): grad_all = lax.all_gather(row_grad, 'section', axis=0, tiled=True)  34.8 us
    all_to_all x1, waiting for transfers between devices, on_device(): weight_pieces = lax.all_to_all(weight_parts, 'joint', 0, 0, tiled=True)  30.3 us
    dot_general x1, matrix products, joint_backward(): lax.dot_general(logit_grad, output_proj, (((1,), (1,)), ((), ())), prefer...  12.3 us
    all_to_all x1, blocking collectives, route_rows(): return lax.all_to_all(picked, axis, 0, 0, tiled=True)  11.5 us
    all_to_all x2, starting transfers between devices, route_rows(): spread = lax.all_to_all(payload, axis, 0, 0, tiled=True)  10.7 us
    broadcast_in_dim x3, local copies, waits for them, and re-layouts, joint_backward(): jnp.where(vocab_iota == token_full[None, :, None], label_full[:, :, None]...  10.4 us
  transfers between devices with their start and end apart: 10, of which 8 were waited for; matrix products, arithmetic and copies ran while one was open for 10% of the time, Pallas kernels for 0%

profile of v5, /device:TPU:2, one launch (start us, length us, event | category | flops | bytes accessed | tf_op | source)
XLA Modules:
  0.0 462.3 jit_solution(16008175747552081733)
XLA Ops:
  11.8 48.1 %all-gather.3.cloned.1.call-done = bf16[1024,1536]{1,0:T(8,128)(2,1)} async-done(((bf16[128,1536]{1,0:T(8,128)(2,1)}), bf16[1024,1536]{1,0:T(8,128)(2,1)}) %all-gather.3.cloned.1.call-update) | async-done | bytes 3145744 | tf_op jit(solution)/shard_map/all_gather | solution.py:273
  59.9 4.0 fusion.82
  63.9 4.5 convolution_multiply_fusion
  68.4 4.9 %all-to-all-start = ((f32[8,128,1536]{2,1,0:T(8,128)}), f32[8,128,1536]{2,1,0:T(8,128)}, u32[]{:S(2)}, u32[]{:S(2)}) async-start(f32[8,128,1536]{2,1,0:T(8,128)} %bitcast.113), calls=%async_computation | async-start | bytes 12582912 | tf_op jit(solution)/shard_map/all_to_all | solution.py:276
  88.4 126.0 %all-to-all-done = f32[8,128,1536]{2,1,0:T(8,128)} async-done(((f32[8,128,1536]{2,1,0:T(8,128)}), f32[8,128,1536]{2,1,0:T(8,128)}, u32[]{:S(2)}, u32[]{:S(2)}) %all-to-all-start) | async-done | bytes 6291488 | tf_op jit(solution)/shard_map/all_to_all | solution.py:276
  214.4 7.4 %all-to-all-start.3 = ((bf16[32,4,640]{2,1,0:T(4,128)(2,1)}), bf16[32,4,640]{2,1,0:T(4,128)(2,1)S(1)}, u32[]{:S(2)}, u32[]{:S(2)}) async-start(bf16[32,4,640]{2,1,0:T(4,128)(2,1)} %all_to_all.47), calls=%async_computation.3 | async-start | bytes 327680 | tf_op jit(solution)/shard_map/all_to_all | solution.py:302
  228.6 5.7 %all-to-all-start.1 = ((bf16[32,4,640]{2,1,0:T(4,128)(2,1)}), bf16[32,4,640]{2,1,0:T(4,128)(2,1)}, u32[]{:S(2)}, u32[]{:S(2)}) async-start(bf16[32,4,640]{2,1,0:T(4,128)(2,1)} %all_to_all.44), calls=%async_computation.1 | async-start | bytes 327680 | tf_op jit(solution)/shard_map/all_to_all | solution.py:243
  239.5 6.8 %broadcast_in_dim.329 = pred[512,4096]{1,0:T(32,128)(4,1)} reshape(pred[128,4,4096]{2,1,0:T(4,128)(4,1)} %broadcast_in_dim.328) | data formatting | bytes 4194304 | tf_op jit(solution)/shard_map/jit(_where)/broadcast_in_dim | solution.py:184
  248.9 7.4 %all-to-all-start.2 = ((bf16[32,4,640]{2,1,0:T(4,128)(2,1)}), bf16[32,4,640]{2,1,0:T(4,128)(2,1)}, u32[]{:S(2)}, u32[]{:S(2)}) async-start(bf16[32,4,640]{2,1,0:T(4,128)(2,1)} %broadcast_select_fusion.1), calls=%async_computation.2 | async-start | bytes 327680 | tf_op jit(solution)/shard_map/all_to_all | solution.py:246
  257.7 5.5 %all-to-all-done.2 = bf16[32,4,640]{2,1,0:T(4,128)(2,1)} async-done(((bf16[32,4,640]{2,1,0:T(4,128)(2,1)}), bf16[32,4,640]{2,1,0:T(4,128)(2,1)}, u32[]{:S(2)}, u32[]{:S(2)}) %all-to-all-start.2) | async-done | bytes 163872 | tf_op jit(solution)/shard_map/all_to_all | solution.py:246
  267.5 9.4 %exponential_reduce_fusion = (f32[512]{0:T(512)S(1)}, f32[512,4096]{1,0:T(8,128)}) fusion(f32[4096]{0:T(1024)} %param.23, bf16[512,640]{1,0:T(8,128)(2,1)} %convert_element_type.87, bf16[640,4096]{1,0:T(8,128)(2,1)} %param.22), kind=kOutput, calls=%fused_computation.6 | convolution fusion | flops 2688548352 | bytes 14305280 | tf_op jit(solution)/shard_map/dot_general | solution.py:158
  276.9 9.8 %reshape.837 = f32[128,4,4096]{2,1,0:T(4,128)} reshape(f32[512,4096]{1,0:T(8,128)} %get-tuple-element.24) | data formatting | bytes 16777216 | tf_op jit(solution)/shard_map/reshape | solution.py:165
  287.7 5.5 %gather_fusion.1 = f32[384]{0:T(512)S(1)} fusion(f32[128,3,4096]{2,1,0:T(4,128)} %bitcast.112, s32[384]{0:T(512)S(1)} %reshape.867), kind=kCustom, calls=%fused_computation.3 | custom fusion | bytes 7680 | tf_op jit(solution)/shard_map/jit(take_along_axis)/gather | solution.py:171
  305.2 7.4 %all-to-all-done.4 = f32[8,4,4]{1,2,0:T(4,128)S(1)} async-done(((f32[8,4,4]{1,2,0:T(4,128)}), f32[8,4,4]{1,2,0:T(4,128)S(1)}, u32[]{:S(2)}, u32[]{:S(2)}) %all-to-all-start.4) | async-done | bytes 544 | tf_op jit(solution)/shard_map/all_to_all | solution.py:321
  318.3 12.3 %fusion.2 = f32[512,640]{1,0:T(8,128)} fusion(bf16[640,4096]{1,0:T(8,128)(2,1)} %param.22, pred[512,4096]{1,0:T(32,128)(4,1)} %broadcast_in_dim.329, f32[512,4096]{1,0:T(8,128)} %get-tuple-element.24, f32[512]{0:T(512)S(1)} %broadcast_in_dim.330, f32[512]{0:T(512)S(1)} %neg.26, f32[512]{0:T(512)S(1)} %mul.131, f32[512]{0:T(512)S(1)} %get-tuple-element.23, ...), kind=kOutput, calls=%fused_computation.18 | convolution fusion | flops 2702442496 | bytes 17707008 | tf_op jit(solution)/shard_map/dot_general | solution.py:187
  336.2 5.0 %all-to-all-start.5 = ((bf16[32,4,640]{2,1,0:T(4,128)(2,1)}), bf16[32,4,640]{2,1,0:T(4,128)(2,1)S(1)}, u32[]{:S(2)}, u32[]{:S(2)}) async-start(bf16[32,4,640]{2,1,0:T(4,128)(2,1)} %convert_element_type.91), calls=%async_computation.5 | async-start | bytes 327680 | tf_op jit(solution)/shard_map/all_to_all | solution.py:243
  341.3 6.8 %all-to-all-done.5 = bf16[32,4,640]{2,1,0:T(4,128)(2,1)S(1)} async-done(((bf16[32,4,640]{2,1,0:T(4,128)(2,1)}), bf16[32,4,640]{2,1,0:T(4,128)(2,1)S(1)}, u32[]{:S(2)}, u32[]{:S(2)}) %all-to-all-start.5) | async-done | bytes 163872 | tf_op jit(solution)/shard_map/all_to_all | solution.py:243
  349.0 11.5 %all_to_all.64 = bf16[32,4,640]{2,1,0:T(4,128)(2,1)S(1)} all-to-all(bf16[32,4,640]{2,1,0:T(4,128)(2,1)S(1)} %broadcast_select_fusion), channel_id=1, replica_groups=mesh['section'=8,'joint'=32] {'joint'}, dimensions={0} | all-to-all | bytes 327680 | tf_op jit(solution)/shard_map/all_to_all | solution.py:246
  363.2 3.6 all-to-all-start.8
  366.8 34.8 %all-gather.5.cloned.1.call-done = bf16[1024,1536]{1,0:T(8,128)(2,1)} async-done(((bf16[128,1536]{1,0:T(8,128)(2,1)}), bf16[1024,1536]{1,0:T(8,128)(2,1)}) %all-gather.5.cloned.1.call-update) | async-done | bytes 3145744 | tf_op jit(solution)/shard_map/all_gather | solution.py:343
  401.6 7.1 %convolution_convert_fusion = bf16[1536,384]{1,0:T(8,128)(2,1)S(1)} fusion(bf16[1024,1536]{1,0:T(8,128)(2,1)} %all-gather.3.cloned.1.call-done, f32[1024,384]{1,0:T(8,128)} %copy-done.20, bf16[1024,1536]{1,0:T(8,128)(2,1)} %all-gather.5.cloned.1.call-done, bf16[384,1536]{1,0:T(8,128)(2,1)} %param.17), kind=kOutput, calls=%fused_computation.13 | convolution fusion | flops 2420441088 | bytes 10223616 | tf_op jit(solution)/shard_map/dot_general | solution.py:351
  408.7 4.3 fusion.1
  414.6 7.3 %all-to-all-start.7 = ((bf16[32,48,768]{2,1,0:T(8,128)(2,1)}), bf16[32,48,768]{2,1,0:T(8,128)(2,1)}, u32[]{:S(2)}, u32[]{:S(2)}) async-start(bf16[32,48,768]{2,1,0:T(8,128)(2,1)} %pad_maximum_fusion), calls=%async_computation.7 | async-start | bytes 4718592 | tf_op jit(solution)/shard_map/all_to_all | solution.py:358
  422.4 30.3 %all-to-all-done.7 = bf16[32,48,768]{2,1,0:T(8,128)(2,1)} async-done(((bf16[32,48,768]{2,1,0:T(8,128)(2,1)}), bf16[32,48,768]{2,1,0:T(8,128)(2,1)}, u32[]{:S(2)}, u32[]{:S(2)}) %all-to-all-start.7) | async-done | bytes 2359328 | tf_op jit(solution)/shard_map/all_to_all | solution.py:358
  (252 shorter events, 70.1 us)
Async XLA Ops:
  7.2 218.5 %copy-start = (bf16[1536,640]{1,0:T(8,128)(2,1)S(1)}, bf16[1536,640]{1,0:T(8,128)(2,1)}, u32[]{:S(2)}) copy-start(bf16[1536,640]{1,0:T(8,128)(2,1)} %param.18) | copy-start | bytes 5898244
  7.2 52.7 %all-gather.3.cloned.1.call-start = ((), (), s32[]{:S(2)}) async-start(), calls=%async_computation.9 | async-start | bytes 3538944 | tf_op jit(solution)/shard_map/all_gather | solution.py:273
  11.8 52.1 %copy-start.15 = (bf16[384,1536]{1,0:T(8,128)(2,1)S(1)}, bf16[384,1536]{1,0:T(8,128)(2,1)}, u32[]{:S(2)}) copy-start(bf16[384,1536]{1,0:T(8,128)(2,1)} %param.17) | copy-start | bytes 3538948
  68.4 7.6 %copy-start.3 = (s32[32,3]{0,1:T(4,128)S(1)}, s32[32,3]{0,1:T(4,128)}, u32[]{:S(2)}) copy-start(s32[32,3]{0,1:T(4,128)} %param.26) | copy-start | bytes 1156
  68.4 9.8 %copy-start.2 = (bf16[128,640]{1,0:T(8,128)(2,1)S(1)}, bf16[128,640]{1,0:T(8,128)(2,1)}, u32[]{:S(2)}) copy-start(bf16[128,640]{1,0:T(8,128)(2,1)} %param.19) | copy-start | bytes 491524
  68.4 10.8 %copy-start.16 = (s32[32]{0:T(128)S(1)}, s32[32]{0:T(128)}, u32[]{:S(2)}) copy-start(s32[32]{0:T(128)} %param.24) | copy-start | bytes 388
  68.4 11.4 %copy-start.17 = (s32[32]{0:T(128)S(1)}, s32[32]{0:T(128)}, u32[]{:S(2)}) copy-start(s32[32]{0:T(128)} %param.25) | copy-start | bytes 388
  68.4 19.3 %copy-start.4 = (f32[2,640]{1,0:T(2,128)S(1)}, f32[2,640]{1,0:T(2,128)}, u32[]{:S(2)}) copy-start(f32[2,640]{1,0:T(2,128)} %param.20) | copy-start | bytes 15364
  68.4 146.0 %all-to-all-start = ((f32[8,128,1536]{2,1,0:T(8,128)}), f32[8,128,1536]{2,1,0:T(8,128)}, u32[]{:S(2)}, u32[]{:S(2)}) async-start(f32[8,128,1536]{2,1,0:T(8,128)} %bitcast.113), calls=%async_computation | async-start | bytes 12582912 | tf_op jit(solution)/shard_map/all_to_all | solution.py:276
  214.4 14.3 %all-to-all-start.3 = ((bf16[32,4,640]{2,1,0:T(4,128)(2,1)}), bf16[32,4,640]{2,1,0:T(4,128)(2,1)S(1)}, u32[]{:S(2)}, u32[]{:S(2)}) async-start(bf16[32,4,640]{2,1,0:T(4,128)(2,1)} %all_to_all.47), calls=%async_computation.3 | async-start | bytes 327680 | tf_op jit(solution)/shard_map/all_to_all | solution.py:302
  228.6 17.8 %all-to-all-start.1 = ((bf16[32,4,640]{2,1,0:T(4,128)(2,1)}), bf16[32,4,640]{2,1,0:T(4,128)(2,1)}, u32[]{:S(2)}, u32[]{:S(2)}) async-start(bf16[32,4,640]{2,1,0:T(4,128)(2,1)} %all_to_all.44), calls=%async_computation.1 | async-start | bytes 327680 | tf_op jit(solution)/shard_map/all_to_all | solution.py:243
  239.5 8.5 %copy-start.12 = (pred[32]{0:T(512)(128)(4,1)S(1)}, pred[32]{0:T(512)(128)(4,1)}, u32[]{:S(2)}) copy-start(pred[32]{0:T(512)(128)(4,1)} %compare_and_fusion.1) | copy-start | bytes 100
  248.9 14.3 %all-to-all-start.2 = ((bf16[32,4,640]{2,1,0:T(4,128)(2,1)}), bf16[32,4,640]{2,1,0:T(4,128)(2,1)}, u32[]{:S(2)}, u32[]{:S(2)}) async-start(bf16[32,4,640]{2,1,0:T(4,128)(2,1)} %broadcast_select_fusion.1), calls=%async_computation.2 | async-start | bytes 327680 | tf_op jit(solution)/shard_map/all_to_all | solution.py:246
  287.7 6.0 %copy-start.7 = (s32[3]{0:T(128)S(1)}, s32[3]{0:T(128)}, u32[]{:S(2)}) copy-start(s32[3]{0:T(128)} %copy-done.6) | copy-start | bytes 40
  293.2 20.6 %copy-start.11 = (pred[8]{0:T(512)(128)(4,1)S(1)}, pred[8]{0:T(512)(128)(4,1)}, u32[]{:S(2)}) copy-start(pred[8]{0:T(512)(128)(4,1)} %iota_compare_fusion.16) | copy-start | bytes 28
  293.2 20.8 %copy-start.10 = (pred[8]{0:T(512)(128)(4,1)S(1)}, pred[8]{0:T(512)(128)(4,1)}, u32[]{:S(2)}) copy-start(pred[8]{0:T(512)(128)(4,1)} %iota_compare_fusion.17) | copy-start | bytes 28
  293.2 22.7 %copy-start.5 = (f32[4]{0:T(128)S(1)}, f32[4]{0:T(128)}, u32[]{:S(2)}) copy-start(f32[4]{0:T(128)} %compare_select_fusion.2) | copy-start | bytes 52
  301.5 11.0 %all-to-all-start.4 = ((f32[8,4,4]{1,2,0:T(4,128)}), f32[8,4,4]{1,2,0:T(4,128)S(1)}, u32[]{:S(2)}, u32[]{:S(2)}) async-start(f32[8,4,4]{1,2,0:T(4,128)} %broadcast_in_dim.320), calls=%async_computation.4 | async-start | bytes 32768 | tf_op jit(solution)/shard_map/all_to_all | solution.py:321
  330.6 10.6 %copy-start.19 = (s32[32]{0:T(128)S(1)}, s32[32]{0:T(128)}, u32[]{:S(2)}) copy-start(s32[32]{0:T(128)} %param.27) | copy-start | bytes 388
  330.6 10.6 %copy-start.14 = (s32[32]{0:T(128)S(1)}, s32[32]{0:T(128)}, u32[]{:S(2)}) copy-start(s32[32]{0:T(128)} %copy-done.13) | copy-start | bytes 388
  336.2 11.9 %all-to-all-start.5 = ((bf16[32,4,640]{2,1,0:T(4,128)(2,1)}), bf16[32,4,640]{2,1,0:T(4,128)(2,1)S(1)}, u32[]{:S(2)}, u32[]{:S(2)}) async-start(bf16[32,4,640]{2,1,0:T(4,128)(2,1)} %convert_element_type.91), calls=%async_computation.5 | async-start | bytes 327680 | tf_op jit(solution)/shard_map/all_to_all | solution.py:243
  341.2 60.4 %all-gather.5.cloned.1.call-start = ((), (), s32[]{:S(2)}) async-start(), calls=%async_computation.10 | async-start | bytes 3538944 | tf_op jit(solution)/shard_map/all_gather | solution.py:343
  363.2 51.3 %all-to-all-start.8 = ((f32[8,4,80]{2,1,0:T(4,128)}), f32[8,4,80]{2,1,0:T(4,128)S(1)}, u32[]{:S(2)}, u32[]{:S(2)}) async-start(f32[8,4,80]{2,1,0:T(4,128)} %copy.173), calls=%async_computation.8 | async-start | bytes 32768 | tf_op jit(solution)/shard_map/all_to_all | solution.py:366
  414.6 38.2 %all-to-all-start.7 = ((bf16[32,48,768]{2,1,0:T(8,128)(2,1)}), bf16[32,48,768]{2,1,0:T(8,128)(2,1)}, u32[]{:S(2)}, u32[]{:S(2)}) async-start(bf16[32,48,768]{2,1,0:T(8,128)(2,1)} %pad_maximum_fusion), calls=%async_computation.7 | async-start | bytes 4718592 | tf_op jit(solution)/shard_map/all_to_all | solution.py:358
  (7 other events, 21.8 us)
Sparse Core Ops, SparseCore 0:
  11.9 47.9 all-gather.2
  362.7 38.9 all-gather.4

commit v6 on v5

--- a/solution.py
+++ b/solution.py
@@ -273,14 +273,12 @@
     gathered = lax.all_gather(normed_in, "section", axis=0, tiled=True)
     pre_hidden = jnp.dot(gathered, up_weight, preferred_element_type=jnp.float32)
     hidden = jax.nn.silu(pre_hidden).astype(jnp.bfloat16)
-    output_pieces = lax.all_to_all(
+    encoded = own_rows + lax.psum_scatter(
         0.5 * jnp.dot(hidden, down_weight, preferred_element_type=jnp.float32),
         "section",
-        0,
-        0,
+        scatter_dimension=0,
         tiled=True,
     )
-    encoded = own_rows + jnp.sum(output_pieces.reshape(section_count, block_len, -1), axis=0)
     unit_rows, inv_scale = layer_norm(encoded)
     frame_part = jnp.dot(
         unit_rows.astype(jnp.bfloat16), encoder_proj, preferred_element_type=jnp.float32

time: 465 us -> 388 us (0.83)
  waiting for transfers between devices: 261 us -> 184 us
    all_to_all x1 -> x0, waiting for transfers between devices: 126 us -> none  [on_device(): lax.all_to_all(0.5 * jnp.dot(hidden, down_weight, preferred_element_type=...]
    reduce_scatter x0 -> x1, waiting for transfers between devices: none -> 50.8 us  [on_device(): lax.psum_scatter(0.5 * jnp.dot(hidden, down_weight, preferred_element_typ...]
    all_to_all x1 -> x0, starting transfers between devices: 4.88 us -> none  [on_device(): lax.all_to_all(0.5 * jnp.dot(hidden, down_weight, preferred_element_type=...]
  transfers between devices with their start and end apart: 10 -> 10, of which waited for: 8 -> 7; matrix products, arithmetic and copies ran while one was open for 10% -> 11% of each run, Pallas kernels for 0% -> 0%
where the time goes in v6:
time: 388 us; the launch traced here: 385 us
  waiting for transfers between devices  184 us (47%)
  local copies, waits for them, and re-layouts  48.1 us (12%)
  matrix products  44.7 us (12%)
  starting transfers between devices  42.4 us (11%)
  other arithmetic  37.7 us (10%)
  between operations  16.5 us (4%)
  blocking collectives  11.5 us (3%)
    reduce_scatter x1, waiting for transfers between devices, on_device(): lax.psum_scatter(0.5 * jnp.dot(hidden, down_weight, preferred_element_typ...  50.8 us
    all_gather x1, waiting for transfers between devices, on_device(): gathered = lax.all_gather(normed_in, 'section', axis=0, tiled=True)  48 us
    all_gather x1, waiting for transfers between devices, on_device(): grad_all = lax.all_gather(row_grad, 'section', axis=0, tiled=True)  34.8 us
    all_to_all x1, waiting for transfers between devices, on_device(): weight_pieces = lax.all_to_all(weight_parts, 'joint', 0, 0, tiled=True)  30.3 us
    dot_general x1, matrix products, joint_backward(): lax.dot_general(logit_grad, output_proj, (((1,), (1,)), ((), ())), prefer...  12.3 us
    all_to_all x2, starting transfers between devices, route_rows(): spread = lax.all_to_all(payload, axis, 0, 0, tiled=True)  12.2 us
    all_to_all x1, blocking collectives, route_rows(): return lax.all_to_all(picked, axis, 0, 0, tiled=True)  11.5 us
    broadcast_in_dim x3, local copies, waits for them, and re-layouts, joint_backward(): jnp.where(vocab_iota == token_full[None, :, None], label_full[:, :, None]...  10.4 us
  transfers between devices with their start and end apart: 10, of which 7 were waited for; matrix products, arithmetic and copies ran while one was open for 11% of the time, Pallas kernels for 0%

profile of v6, /device:TPU:2, one launch (start us, length us, event | category | flops | bytes accessed | tf_op | source)
XLA Modules:
  0.0 385.0 jit_solution(3007359183366740021)
XLA Ops:
  11.8 48.0 %all-gather.3.cloned.1.call-done = bf16[1024,1536]{1,0:T(8,128)(2,1)} async-done(((bf16[128,1536]{1,0:T(8,128)(2,1)}), bf16[1024,1536]{1,0:T(8,128)(2,1)}) %all-gather.3.cloned.1.call-update) | async-done | bytes 3145744 | tf_op jit(solution)/shard_map/all_gather | solution.py:273
  59.9 4.0 %fusion.82 = f32[1024,384]{1,0:T(8,128)S(1)} fusion(bf16[1024,1536]{1,0:T(8,128)(2,1)} %all-gather.3.cloned.1.call-done, bf16[1536,384]{1,0:T(8,128)(2,1)} %param.16), kind=kOutput, calls=%fused_computation.250 | convolution fusion | flops 1207959552 | bytes 5898240 | tf_op jit(solution)/shard_map/dot_general | solution.py:274
  65.1 4.5 %convolution_multiply_fusion = f32[1024,1536]{1,0:T(8,128)} fusion(bf16[384,1536]{1,0:T(8,128)(2,1)S(1)} %copy-done.17, f32[1024,384]{1,0:T(8,128)S(1)} %fusion.82), kind=kOutput, calls=%fused_computation.9 | convolution fusion | flops 1211498496 | bytes 9043968 | tf_op jit(solution)/shard_map/dot_general | solution.py:277
  72.8 7.4 %all-to-all-start.2 = ((bf16[32,4,640]{2,1,0:T(4,128)(2,1)}), bf16[32,4,640]{2,1,0:T(4,128)(2,1)S(1)}, u32[]{:S(2)}, u32[]{:S(2)}) async-start(bf16[32,4,640]{2,1,0:T(4,128)(2,1)} %all_to_all.39), calls=%async_computation.3 | async-start | bytes 327680 | tf_op jit(solution)/shard_map/all_to_all | solution.py:300
  92.7 50.8 %reduce-scatter.2.cloned.1.call-done = f32[128,1536]{1,0:T(8,128)} async-done(((f32[1024,1536]{1,0:T(8,128)}), f32[128,1536]{1,0:T(8,128)}) %reduce-scatter.2.cloned.1.call-update) | async-done | bytes 786448 | tf_op jit(solution)/shard_map/reduce_scatter | solution.py:276
  147.6 7.5 %all-to-all-start = ((bf16[32,4,640]{2,1,0:T(4,128)(2,1)}), bf16[32,4,640]{2,1,0:T(4,128)(2,1)}, u32[]{:S(2)}, u32[]{:S(2)}) async-start(bf16[32,4,640]{2,1,0:T(4,128)(2,1)} %all_to_all.36), calls=%async_computation.1 | async-start | bytes 327680 | tf_op jit(solution)/shard_map/all_to_all | solution.py:243
  160.1 6.8 %broadcast_in_dim.329 = pred[512,4096]{1,0:T(32,128)(4,1)} reshape(pred[128,4,4096]{2,1,0:T(4,128)(4,1)} %broadcast_in_dim.328) | data formatting | bytes 4194304 | tf_op jit(solution)/shard_map/jit(_where)/broadcast_in_dim | solution.py:184
  169.5 7.4 %all-to-all-start.1 = ((bf16[32,4,640]{2,1,0:T(4,128)(2,1)}), bf16[32,4,640]{2,1,0:T(4,128)(2,1)}, u32[]{:S(2)}, u32[]{:S(2)}) async-start(bf16[32,4,640]{2,1,0:T(4,128)(2,1)} %broadcast_select_fusion.1), calls=%async_computation.2 | async-start | bytes 327680 | tf_op jit(solution)/shard_map/all_to_all | solution.py:246
  178.3 5.5 %all-to-all-done.1 = bf16[32,4,640]{2,1,0:T(4,128)(2,1)} async-done(((bf16[32,4,640]{2,1,0:T(4,128)(2,1)}), bf16[32,4,640]{2,1,0:T(4,128)(2,1)}, u32[]{:S(2)}, u32[]{:S(2)}) %all-to-all-start.1) | async-done | bytes 163872 | tf_op jit(solution)/shard_map/all_to_all | solution.py:246
  188.2 9.4 %exponential_reduce_fusion = (f32[512]{0:T(512)S(1)}, f32[512,4096]{1,0:T(8,128)}) fusion(f32[4096]{0:T(1024)} %param.23, bf16[512,640]{1,0:T(8,128)(2,1)} %convert_element_type.87, bf16[640,4096]{1,0:T(8,128)(2,1)} %param.22), kind=kOutput, calls=%fused_computation.6 | convolution fusion | flops 2688548352 | bytes 14305280 | tf_op jit(solution)/shard_map/dot_general | solution.py:158
  197.6 9.8 %reshape.833 = f32[128,4,4096]{2,1,0:T(4,128)} reshape(f32[512,4096]{1,0:T(8,128)} %get-tuple-element.24) | data formatting | bytes 16777216 | tf_op jit(solution)/shard_map/reshape | solution.py:165
  208.4 5.7 %gather_fusion.1 = f32[384]{0:T(512)S(1)} fusion(f32[128,3,4096]{2,1,0:T(4,128)} %bitcast.111, s32[384]{0:T(512)S(1)} %reshape.863), kind=kCustom, calls=%fused_computation.3 | custom fusion | bytes 7680 | tf_op jit(solution)/shard_map/jit(take_along_axis)/gather | solution.py:171
  222.4 4.3 %all-to-all-start.3 = ((f32[8,4,4]{1,2,0:T(4,128)}), f32[8,4,4]{1,2,0:T(4,128)S(1)}, u32[]{:S(2)}, u32[]{:S(2)}) async-start(f32[8,4,4]{1,2,0:T(4,128)} %broadcast_in_dim.320), calls=%async_computation.4 | async-start | bytes 32768 | tf_op jit(solution)/shard_map/all_to_all | solution.py:319
  226.8 7.7 %all-to-all-done.3 = f32[8,4,4]{1,2,0:T(4,128)S(1)} async-done(((f32[8,4,4]{1,2,0:T(4,128)}), f32[8,4,4]{1,2,0:T(4,128)S(1)}, u32[]{:S(2)}, u32[]{:S(2)}) %all-to-all-start.3) | async-done | bytes 544 | tf_op jit(solution)/shard_map/all_to_all | solution.py:319
  241.5 12.3 %fusion.2 = f32[512,640]{1,0:T(8,128)} fusion(bf16[640,4096]{1,0:T(8,128)(2,1)} %param.22, pred[512,4096]{1,0:T(32,128)(4,1)} %broadcast_in_dim.329, f32[512,4096]{1,0:T(8,128)} %get-tuple-element.24, f32[512]{0:T(512)S(1)} %broadcast_in_dim.330, f32[512]{0:T(512)S(1)} %neg.26, f32[512]{0:T(512)S(1)} %mul.131, f32[512]{0:T(512)S(1)} %copy-done.7, ...), kind=kOutput, calls=%fused_computation.18 | convolution fusion | flops 2702442496 | bytes 17707008 | tf_op jit(solution)/shard_map/dot_general | solution.py:187
  259.4 4.8 %all-to-all-start.4 = ((bf16[32,4,640]{2,1,0:T(4,128)(2,1)}), bf16[32,4,640]{2,1,0:T(4,128)(2,1)S(1)}, u32[]{:S(2)}, u32[]{:S(2)}) async-start(bf16[32,4,640]{2,1,0:T(4,128)(2,1)} %convert_element_type.91), calls=%async_computation.5 | async-start | bytes 327680 | tf_op jit(solution)/shard_map/all_to_all | solution.py:243
  264.3 6.8 %all-to-all-done.4 = bf16[32,4,640]{2,1,0:T(4,128)(2,1)S(1)} async-done(((bf16[32,4,640]{2,1,0:T(4,128)(2,1)}), bf16[32,4,640]{2,1,0:T(4,128)(2,1)S(1)}, u32[]{:S(2)}, u32[]{:S(2)}) %all-to-all-start.4) | async-done | bytes 163872 | tf_op jit(solution)/shard_map/all_to_all | solution.py:243
  272.0 11.5 %all_to_all.55 = bf16[32,4,640]{2,1,0:T(4,128)(2,1)S(1)} all-to-all(bf16[32,4,640]{2,1,0:T(4,128)(2,1)S(1)} %broadcast_select_fusion), channel_id=1, replica_groups=mesh['section'=8,'joint'=32] {'joint'}, dimensions={0} | all-to-all | bytes 327680 | tf_op jit(solution)/shard_map/all_to_all | solution.py:246
  286.2 3.6 all-to-all-start.7
  289.9 34.8 %all-gather.5.cloned.1.call-done = bf16[1024,1536]{1,0:T(8,128)(2,1)} async-done(((bf16[128,1536]{1,0:T(8,128)(2,1)}), bf16[1024,1536]{1,0:T(8,128)(2,1)}) %all-gather.5.cloned.1.call-update) | async-done | bytes 3145744 | tf_op jit(solution)/shard_map/all_gather | solution.py:341
  324.6 7.1 %convolution_convert_fusion = bf16[1536,384]{1,0:T(8,128)(2,1)S(1)} fusion(bf16[1024,1536]{1,0:T(8,128)(2,1)} %all-gather.3.cloned.1.call-done, f32[1024,384]{1,0:T(8,128)} %copy-done.22, bf16[1024,1536]{1,0:T(8,128)(2,1)} %all-gather.5.cloned.1.call-done, bf16[384,1536]{1,0:T(8,128)(2,1)} %param.17), kind=kOutput, calls=%fused_computation.13 | convolution fusion | flops 2420441088 | bytes 10223616 | tf_op jit(solution)/shard_map/dot_general | solution.py:349
  331.7 4.2 %fusion.1 = bf16[1536,384]{1,0:T(8,128)(2,1)S(1)} fusion(bf16[1024,1536]{1,0:T(8,128)(2,1)} %all-gather.5.cloned.1.call-done, f32[1024,384]{1,0:T(8,128)} %copy-done.22), kind=kOutput, calls=%fused_computation.12 | convolution fusion | flops 1211105280 | bytes 5898240 | tf_op jit(solution)/shard_map/dot_general | solution.py:352
  337.6 7.3 %all-to-all-start.6 = ((bf16[32,48,768]{2,1,0:T(8,128)(2,1)}), bf16[32,48,768]{2,1,0:T(8,128)(2,1)}, u32[]{:S(2)}, u32[]{:S(2)}) async-start(bf16[32,48,768]{2,1,0:T(8,128)(2,1)} %pad_maximum_fusion), calls=%async_computation.7 | async-start | bytes 4718592 | tf_op jit(solution)/shard_map/all_to_all | solution.py:356
  345.4 30.3 %all-to-all-done.6 = bf16[32,48,768]{2,1,0:T(8,128)(2,1)} async-done(((bf16[32,48,768]{2,1,0:T(8,128)(2,1)}), bf16[32,48,768]{2,1,0:T(8,128)(2,1)}, u32[]{:S(2)}, u32[]{:S(2)}) %all-to-all-start.6) | async-done | bytes 2359328 | tf_op jit(solution)/shard_map/all_to_all | solution.py:356
  (256 shorter events, 66.9 us)
Async XLA Ops:
  7.2 139.1 %copy-start = (bf16[1536,640]{1,0:T(8,128)(2,1)S(1)}, bf16[1536,640]{1,0:T(8,128)(2,1)}, u32[]{:S(2)}) copy-start(bf16[1536,640]{1,0:T(8,128)(2,1)} %param.18) | copy-start | bytes 5898244
  7.2 52.7 %all-gather.3.cloned.1.call-start = ((), (), s32[]{:S(2)}) async-start(), calls=%async_computation.9 | async-start | bytes 3538944 | tf_op jit(solution)/shard_map/all_gather | solution.py:273
  11.8 53.3 %copy-start.17 = (bf16[384,1536]{1,0:T(8,128)(2,1)S(1)}, bf16[384,1536]{1,0:T(8,128)(2,1)}, u32[]{:S(2)}) copy-start(bf16[384,1536]{1,0:T(8,128)(2,1)} %param.17) | copy-start | bytes 3538948
  11.8 131.8 %reduce-scatter.2.cloned.1.call-start = ((), (), s32[]{:S(2)}) async-start(), calls=%async_computation.10 | async-start | bytes 7077888 | tf_op jit(solution)/shard_map/reduce_scatter | solution.py:276
  69.6 13.9 %copy-start.18 = (s32[32]{0:T(128)S(1)}, s32[32]{0:T(128)}, u32[]{:S(2)}) copy-start(s32[32]{0:T(128)} %param.24) | copy-start | bytes 388
  69.6 14.5 %copy-start.19 = (s32[32]{0:T(128)S(1)}, s32[32]{0:T(128)}, u32[]{:S(2)}) copy-start(s32[32]{0:T(128)} %param.25) | copy-start | bytes 388
  69.6 22.5 %copy-start.5 = (f32[2,640]{1,0:T(2,128)S(1)}, f32[2,640]{1,0:T(2,128)}, u32[]{:S(2)}) copy-start(f32[2,640]{1,0:T(2,128)} %param.20) | copy-start | bytes 15364
  69.6 73.9 %copy-start.1 = (bf16[1,128,1536]{2,1,0:T(8,128)(2,1)S(1)}, bf16[1,128,1536]{2,1,0:T(8,128)(2,1)}, u32[]{:S(2)}) copy-start(bf16[1,128,1536]{2,1,0:T(8,128)(2,1)} %param.15) | copy-start | bytes 1179652
  72.8 74.7 %all-to-all-start.2 = ((bf16[32,4,640]{2,1,0:T(4,128)(2,1)}), bf16[32,4,640]{2,1,0:T(4,128)(2,1)S(1)}, u32[]{:S(2)}, u32[]{:S(2)}) async-start(bf16[32,4,640]{2,1,0:T(4,128)(2,1)} %all_to_all.39), calls=%async_computation.3 | async-start | bytes 327680 | tf_op jit(solution)/shard_map/all_to_all | solution.py:300
  83.0 9.6 %copy-start.10 = (pred[3]{0:T(512)(128)(4,1)}, pred[3]{0:T(512)(128)(4,1)S(1)}, u32[]{:S(2)}) copy-start(pred[3]{0:T(512)(128)(4,1)S(1)} %broadcast_compare_fusion) | copy-start | bytes 13
  147.6 19.5 %all-to-all-start = ((bf16[32,4,640]{2,1,0:T(4,128)(2,1)}), bf16[32,4,640]{2,1,0:T(4,128)(2,1)}, u32[]{:S(2)}, u32[]{:S(2)}) async-start(bf16[32,4,640]{2,1,0:T(4,128)(2,1)} %all_to_all.36), calls=%async_computation.1 | async-start | bytes 327680 | tf_op jit(solution)/shard_map/all_to_all | solution.py:243
  160.1 8.5 %copy-start.14 = (pred[32]{0:T(512)(128)(4,1)S(1)}, pred[32]{0:T(512)(128)(4,1)}, u32[]{:S(2)}) copy-start(pred[32]{0:T(512)(128)(4,1)} %compare_and_fusion.1) | copy-start | bytes 100
  169.5 14.3 %all-to-all-start.1 = ((bf16[32,4,640]{2,1,0:T(4,128)(2,1)}), bf16[32,4,640]{2,1,0:T(4,128)(2,1)}, u32[]{:S(2)}, u32[]{:S(2)}) async-start(bf16[32,4,640]{2,1,0:T(4,128)(2,1)} %broadcast_select_fusion.1), calls=%async_computation.2 | async-start | bytes 327680 | tf_op jit(solution)/shard_map/all_to_all | solution.py:246
  197.6 16.8 %copy-start.6 = (f32[512]{0:T(512)}, f32[512]{0:T(512)S(1)}, u32[]{:S(2)}) copy-start(f32[512]{0:T(512)S(1)} %get-tuple-element.23) | copy-start | bytes 6148
  214.0 21.7 %copy-start.13 = (pred[8]{0:T(512)(128)(4,1)S(1)}, pred[8]{0:T(512)(128)(4,1)}, u32[]{:S(2)}) copy-start(pred[8]{0:T(512)(128)(4,1)} %iota_compare_fusion.16) | copy-start | bytes 28
  214.0 21.9 %copy-start.12 = (pred[8]{0:T(512)(128)(4,1)S(1)}, pred[8]{0:T(512)(128)(4,1)}, u32[]{:S(2)}) copy-start(pred[8]{0:T(512)(128)(4,1)} %iota_compare_fusion.17) | copy-start | bytes 28
  214.5 26.9 %copy-start.7 = (f32[512]{0:T(512)S(1)}, f32[512]{0:T(512)}, u32[]{:S(2)}) copy-start(f32[512]{0:T(512)} %copy-done.6) | copy-start | bytes 6148
  222.4 12.1 %all-to-all-start.3 = ((f32[8,4,4]{1,2,0:T(4,128)}), f32[8,4,4]{1,2,0:T(4,128)S(1)}, u32[]{:S(2)}, u32[]{:S(2)}) async-start(f32[8,4,4]{1,2,0:T(4,128)} %broadcast_in_dim.320), calls=%async_computation.4 | async-start | bytes 32768 | tf_op jit(solution)/shard_map/all_to_all | solution.py:319
  253.8 10.4 %copy-start.21 = (s32[32]{0:T(128)S(1)}, s32[32]{0:T(128)}, u32[]{:S(2)}) copy-start(s32[32]{0:T(128)} %param.27) | copy-start | bytes 388
  253.8 10.5 %copy-start.16 = (s32[32]{0:T(128)S(1)}, s32[32]{0:T(128)}, u32[]{:S(2)}) copy-start(s32[32]{0:T(128)} %copy-done.15) | copy-start | bytes 388
  259.4 11.7 %all-to-all-start.4 = ((bf16[32,4,640]{2,1,0:T(4,128)(2,1)}), bf16[32,4,640]{2,1,0:T(4,128)(2,1)S(1)}, u32[]{:S(2)}, u32[]{:S(2)}) async-start(bf16[32,4,640]{2,1,0:T(4,128)(2,1)} %convert_element_type.91), calls=%async_computation.5 | async-start | bytes 327680 | tf_op jit(solution)/shard_map/all_to_all | solution.py:243
  264.2 60.4 %all-gather.5.cloned.1.call-start = ((), (), s32[]{:S(2)}) async-start(), calls=%async_computation.11 | async-start | bytes 3538944 | tf_op jit(solution)/shard_map/all_gather | solution.py:341
  286.2 51.3 %all-to-all-start.7 = ((f32[8,4,80]{2,1,0:T(4,128)}), f32[8,4,80]{2,1,0:T(4,128)S(1)}, u32[]{:S(2)}, u32[]{:S(2)}) async-start(f32[8,4,80]{2,1,0:T(4,128)} %copy.173), calls=%async_computation.8 | async-start | bytes 32768 | tf_op jit(solution)/shard_map/all_to_all | solution.py:364
  337.6 38.2 %all-to-all-start.6 = ((bf16[32,48,768]{2,1,0:T(8,128)(2,1)}), bf16[32,48,768]{2,1,0:T(8,128)(2,1)}, u32[]{:S(2)}, u32[]{:S(2)}) async-start(bf16[32,48,768]{2,1,0:T(8,128)(2,1)} %pad_maximum_fusion), calls=%async_computation.7 | async-start | bytes 4718592 | tf_op jit(solution)/shard_map/all_to_all | solution.py:356
  (9 other events, 21.6 us)
Sparse Core Ops, SparseCore 0:
  11.9 47.9 all-gather.2
  69.7 73.7 reduce-scatter.1
  285.7 38.8 all-gather.4
